TPU v7x, 768 devices: a whole 4x8x12 slice. The times are simulated.
768 devices in a mesh: seq: 32 (over y, x), head: 24 (over z, core).
Axes of the slice: x: 4, y: 8, z: 12, core: 2. Of those that a mesh axis runs over, the one named last changes fastest.
Arguments:
- queries: bfloat16 [49152, 12288], P('seq', 'head'), may hold values from -70.26874 to 70.26874
- keys: bfloat16 [49152, 3072], P('seq', 'head'), may hold values from -6 to 6
- values: bfloat16 [49152, 3072], P('seq', 'head'), may hold values from -6 to 6
- file_lengths: int32 [3, 384], replicated, may hold values from 1 to 512, 49152 in all within a row
- owner_of: int32 [32, 32], P('seq'), may hold values from 0 to 31, each once within a row
Outputs:
- owned: bfloat16 [32, 32, 48, 12288], P('seq', None, 'head')
Inputs may be any that keep to these rules, and one draw needn't show every extreme that they name: `owner_of`: row s names, for each of the 32 pieces of 48 tokens of shard s, its owner; each row names every owner once; the assignment is arbitrary.
All inputs are finite; a program needn't handle non-finite values.
Results may differ from a plain program's by a relative error of at most 0.0044.
Values may be sent and summed in bfloat16 or wider, within the bound.
No kernel may reach another device: no remote copies, remote signals or barrier semaphores. Data moves between devices by JAX's collectives and lax.ppermute only.
A program may use at most 32 MiB of HBM per device.

v0:
```python
import math

import jax
import jax.numpy as jnp
from jax import lax
from jax.sharding import PartitionSpec as P

HD = 128
KV_HEADS = 8
FILE_MOST = 512
QROWS = 256


def from_behind(block, axis, distance):
    devices = range(lax.axis_size(axis))
    route = [(i - distance, i) for i in devices if i - distance in devices]
    return lax.ppermute(block, axis, route)


def attend_block(q_block, k_window, v_window, q_doc, k_doc, q_pos, k_pos, scale):
    scores = (
        jnp.einsum("qhgd,khd->hgqk", q_block, k_window, preferred_element_type=jnp.float32) * scale
    )
    allowed = (
        (k_doc[None, :] == q_doc[:, None])
        & (k_pos[None, :] <= q_pos[:, None])
        & (k_pos[None, :] >= 0)
    )
    scores = jnp.where(allowed[None, None, :, :], scores, -jnp.inf)
    row_max = jnp.max(scores, axis=3, keepdims=True)
    expo = jnp.exp(scores - row_max)
    weights = (expo / jnp.sum(expo, axis=3, keepdims=True)).astype(jnp.bfloat16)
    result = jnp.einsum("hgqk,khd->qhgd", weights, v_window, preferred_element_type=jnp.float32)
    return result.astype(jnp.bfloat16)


def stacked_windows(array, block_count, reach):
    tiles = array.reshape((block_count + reach, QROWS) + array.shape[1:])
    return jnp.concatenate([tiles[step : step + block_count] for step in range(reach + 1)], axis=1)


def per_device(queries, keys, values, file_lengths, owner_of):
    tok_rows = queries.shape[0]
    heads_here = keys.shape[1] // HD
    group_size = queries.shape[1] // keys.shape[1]
    shard_count = lax.axis_size("seq")
    offset = lax.axis_index("seq") * tok_rows
    sequence = lax.axis_index("head") * heads_here // KV_HEADS
    earlier = from_behind((keys, values), "seq", 1)
    rim_keys = earlier[0][tok_rows - FILE_MOST :]
    rim_values = earlier[1][tok_rows - FILE_MOST :]
    wide_keys = jnp.concatenate([rim_keys, keys], axis=0).reshape(
        tok_rows + FILE_MOST, heads_here, HD
    )
    wide_values = jnp.concatenate([rim_values, values], axis=0).reshape(
        tok_rows + FILE_MOST, heads_here, HD
    )
    file_count = file_lengths.shape[1]
    batch_pick = (jnp.arange(file_lengths.shape[0], dtype=jnp.int32) == sequence).astype(jnp.int32)
    lengths_here = jnp.sum(file_lengths * batch_pick[:, None], axis=0)
    file_index = jnp.arange(file_count, dtype=jnp.int32)
    upto = (file_index[:, None] <= file_index[None, :]).astype(jnp.int32)
    file_ends = jnp.sum(lengths_here[:, None] * upto, axis=0)
    positions = offset - FILE_MOST + jnp.arange(tok_rows + FILE_MOST, dtype=jnp.int32)
    doc_ids = jnp.sum((file_ends[None, :] <= positions[:, None]).astype(jnp.int32), axis=1)
    scale = 1.0 / math.sqrt(HD)
    block_count = tok_rows // QROWS
    reach = FILE_MOST // QROWS
    q_blocks = queries.reshape(block_count, QROWS, heads_here, group_size, HD)
    k_blocks = stacked_windows(wide_keys, block_count, reach)
    v_blocks = stacked_windows(wide_values, block_count, reach)
    kd_blocks = stacked_windows(doc_ids, block_count, reach)
    kp_blocks = stacked_windows(positions, block_count, reach)
    qd_blocks = doc_ids[FILE_MOST:].reshape(block_count, QROWS)
    qp_blocks = positions[FILE_MOST:].reshape(block_count, QROWS)

    def one_block(operands):
        q_block, k_window, v_window, q_doc, k_doc, q_pos, k_pos = operands
        return attend_block(q_block, k_window, v_window, q_doc, k_doc, q_pos, k_pos, scale)

    blocks = lax.map(
        one_block, (q_blocks, k_blocks, v_blocks, qd_blocks, kd_blocks, qp_blocks, kp_blocks)
    )
    attended = blocks.reshape(tok_rows, heads_here * group_size * HD)
    pieces = attended.reshape(shard_count, tok_rows // shard_count, heads_here * group_size * HD)
    owner_index = jnp.arange(shard_count, dtype=jnp.int32)
    one_hot = (owner_of[0][None, :] == owner_index[:, None]).astype(jnp.bfloat16)
    ordered = jnp.einsum("op,prc->orc", one_hot, pieces, preferred_element_type=jnp.float32).astype(
        jnp.bfloat16
    )
    arrived = lax.all_to_all(
        lax.all_to_all(ordered, "seq", split_axis=0, concat_axis=0, tiled=True),
        "head",
        split_axis=1,
        concat_axis=2,
        tiled=True,
    )
    return arrived[None]


def solution(mesh):
    return jax.shard_map(
        per_device,
        mesh=mesh,
        in_specs=(P("seq", "head"), P("seq", "head"), P("seq", "head"), P(), P("seq", None)),
        out_specs=P("seq", None, "head", None),
        check_vma=False,
    )
```

profile of v0, /device:TPU:1, one launch (start us, length us, event | category | flops | bytes accessed | tf_op | source)
XLA Modules:
  0.0 186.2 jit_solution(8491084056294681200)
XLA Ops:
  0.0 4.1 %collective-permute-start = (bf16[1536,128]{1,0:T(8,128)(2,1)}, bf16[1536,128]{1,0:T(8,128)(2,1)S(1)}, u32[]{:S(2)}, u32[]{:S(2)}) collective-permute-start(bf16[1536,128]{1,0:T(8,128)(2,1)} %param.9), channel_id=1, source_target_pairs={{0,24},{24,48},{48,72},{72,96},{96,120},{120,144},{144,168},{168,1... | collective-permute-start | bytes 1179656 | tf_op jit(solution)/shard_map/ppermute | solution.py:17
  4.1 3.8 %collective-permute-start.1 = (bf16[1536,128]{1,0:T(8,128)(2,1)}, bf16[1536,128]{1,0:T(8,128)(2,1)}, u32[]{:S(2)}, u32[]{:S(2)}) collective-permute-start(bf16[1536,128]{1,0:T(8,128)(2,1)} %param.8), channel_id=1, source_target_pairs={{0,24},{24,48},{48,72},{72,96},{96,120},{120,144},{144,168},{168,1... | collective-permute-start | bytes 1179656 | tf_op jit(solution)/shard_map/ppermute | solution.py:17
  7.9 0.8 multiply_reduce_fusion
  8.7 0.1 select_reduce_fusion
  8.9 0.7 convert_reduce_fusion
  9.7 0.0 copy-start.1
  9.7 2.4 %reshape.177 = bf16[6,256,1,4,128]{4,3,1,0,2:T(4,128)(2,1)S(1)} reshape(bf16[1536,512]{1,0:T(8,128)(2,1)} %param.7) | data formatting | bytes 3145728 | tf_op jit(solution)/shard_map/reshape | solution.py:69
  12.2 0.1 fusion.22
  12.2 1.5 collective-permute-done.1
  13.7 0.9 slice.130
  14.6 0.1 fusion.21
  14.7 1.1 pad_maximum_fusion
  15.8 0.1 pad_maximum_fusion.1
  15.9 31.4 %while.10 = (s32[]{:T(128)}, bf16[6,256,1,4,128]{4,3,1,0,2:T(4,128)(2,1)}, bf16[6,768,1,128]{3,1,0,2:T(8,128)(2,1)}, s32[6,768]{1,0:T(8,128)S(1)}, s32[6,256]{1,...) while((s32[]{:T(128)}, ...), condition=%wide.region_6.7_spmd, body=%wide.region_3.6_spmd.sunk | while | flops 413006592 | bytes 12764793 | solution.py:81
  16.0 0.7 and_and_fusion.2
  16.7 0.1 constant_dynamic-slice_fusion.7
  16.8 0.6 fusion.35
  17.5 0.7 fusion.36
  18.2 2.0 %fusion.37 = bf16[1,256,1,4,128]{1,4,3,2,0:T(8,128)(2,1)S(1)} fusion(f32[4,256]{1,0:T(4,128)S(1)} %fusion.36, f32[4,256]{1,0:T(4,128)S(1)} %get-tuple-element.191, f32[768,256,4]{1,0,2:T(8,128)S(1)} %get-tuple-element.190, pred[256,768]{0,1:T(8,128)(4,1)S(1)} %and_and_fusion.2, bf16[6,768,1,128]{3,1,0,2:T(8,128)(2,1)} %get-tuple-element.214, ...), kind=kOutput, calls=%fused_computation.8.clone.1 | convolution fusion | flops 205389824 | bytes 3809792 | tf_op jit(solution)/shard_map/while/body/eval_jaxpr/hgqk,khd->qhgd/dot_general | solution.py:33
  20.1 0.2 copy.51
  20.3 0.8 constant_dynamic-update-slice_fusion.2
  21.2 0.7 and_and_fusion.2
  22.0 0.1 constant_dynamic-slice_fusion.7
  22.1 0.6 fusion.35
  22.7 0.7 fusion.36
  23.4 2.0 %fusion.37 = bf16[1,256,1,4,128]{1,4,3,2,0:T(8,128)(2,1)S(1)} fusion(f32[4,256]{1,0:T(4,128)S(1)} %fusion.36, f32[4,256]{1,0:T(4,128)S(1)} %get-tuple-element.191, f32[768,256,4]{1,0,2:T(8,128)S(1)} %get-tuple-element.190, pred[256,768]{0,1:T(8,128)(4,1)S(1)} %and_and_fusion.2, bf16[6,768,1,128]{3,1,0,2:T(8,128)(2,1)} %get-tuple-element.214, ...), kind=kOutput, calls=%fused_computation.8.clone.1 | convolution fusion | flops 205389824 | bytes 3809792 | tf_op jit(solution)/shard_map/while/body/eval_jaxpr/hgqk,khd->qhgd/dot_general | solution.py:33
  25.4 0.2 copy.51
  25.6 0.8 constant_dynamic-update-slice_fusion.2
  26.4 0.7 and_and_fusion.2
  27.2 0.1 constant_dynamic-slice_fusion.7
  27.3 0.6 fusion.35
  27.9 0.7 fusion.36
  28.6 2.0 %fusion.37 = bf16[1,256,1,4,128]{1,4,3,2,0:T(8,128)(2,1)S(1)} fusion(f32[4,256]{1,0:T(4,128)S(1)} %fusion.36, f32[4,256]{1,0:T(4,128)S(1)} %get-tuple-element.191, f32[768,256,4]{1,0,2:T(8,128)S(1)} %get-tuple-element.190, pred[256,768]{0,1:T(8,128)(4,1)S(1)} %and_and_fusion.2, bf16[6,768,1,128]{3,1,0,2:T(8,128)(2,1)} %get-tuple-element.214, ...), kind=kOutput, calls=%fused_computation.8.clone.1 | convolution fusion | flops 205389824 | bytes 3809792 | tf_op jit(solution)/shard_map/while/body/eval_jaxpr/hgqk,khd->qhgd/dot_general | solution.py:33
  30.6 0.2 copy.51
  30.8 0.8 constant_dynamic-update-slice_fusion.2
  31.7 0.7 and_and_fusion.2
  32.4 0.1 constant_dynamic-slice_fusion.7
  32.5 0.6 fusion.35
  33.2 0.7 fusion.36
  33.9 2.0 %fusion.37 = bf16[1,256,1,4,128]{1,4,3,2,0:T(8,128)(2,1)S(1)} fusion(f32[4,256]{1,0:T(4,128)S(1)} %fusion.36, f32[4,256]{1,0:T(4,128)S(1)} %get-tuple-element.191, f32[768,256,4]{1,0,2:T(8,128)S(1)} %get-tuple-element.190, pred[256,768]{0,1:T(8,128)(4,1)S(1)} %and_and_fusion.2, bf16[6,768,1,128]{3,1,0,2:T(8,128)(2,1)} %get-tuple-element.214, ...), kind=kOutput, calls=%fused_computation.8.clone.1 | convolution fusion | flops 205389824 | bytes 3809792 | tf_op jit(solution)/shard_map/while/body/eval_jaxpr/hgqk,khd->qhgd/dot_general | solution.py:33
  35.8 0.2 copy.51
  36.0 0.8 constant_dynamic-update-slice_fusion.2
  36.9 0.7 and_and_fusion.2
  37.7 0.1 constant_dynamic-slice_fusion.7
  37.8 0.6 fusion.35
  38.4 0.7 fusion.36
  39.1 2.0 %fusion.37 = bf16[1,256,1,4,128]{1,4,3,2,0:T(8,128)(2,1)S(1)} fusion(f32[4,256]{1,0:T(4,128)S(1)} %fusion.36, f32[4,256]{1,0:T(4,128)S(1)} %get-tuple-element.191, f32[768,256,4]{1,0,2:T(8,128)S(1)} %get-tuple-element.190, pred[256,768]{0,1:T(8,128)(4,1)S(1)} %and_and_fusion.2, bf16[6,768,1,128]{3,1,0,2:T(8,128)(2,1)} %get-tuple-element.214, ...), kind=kOutput, calls=%fused_computation.8.clone.1 | convolution fusion | flops 205389824 | bytes 3809792 | tf_op jit(solution)/shard_map/while/body/eval_jaxpr/hgqk,khd->qhgd/dot_general | solution.py:33
  41.1 0.2 copy.51
  41.3 0.8 constant_dynamic-update-slice_fusion.2
  42.1 0.7 and_and_fusion.2
  42.9 0.1 constant_dynamic-slice_fusion.7
  43.0 0.6 fusion.35
  43.6 0.7 fusion.36
  44.3 2.0 %fusion.37 = bf16[1,256,1,4,128]{1,4,3,2,0:T(8,128)(2,1)S(1)} fusion(f32[4,256]{1,0:T(4,128)S(1)} %fusion.36, f32[4,256]{1,0:T(4,128)S(1)} %get-tuple-element.191, f32[768,256,4]{1,0,2:T(8,128)S(1)} %get-tuple-element.190, pred[256,768]{0,1:T(8,128)(4,1)S(1)} %and_and_fusion.2, bf16[6,768,1,128]{3,1,0,2:T(8,128)(2,1)} %get-tuple-element.214, ...), kind=kOutput, calls=%fused_computation.8.clone.1 | convolution fusion | flops 205389824 | bytes 3809792 | tf_op jit(solution)/shard_map/while/body/eval_jaxpr/hgqk,khd->qhgd/dot_general | solution.py:33
  46.3 0.2 copy.51
  46.5 0.8 constant_dynamic-update-slice_fusion.2
  47.3 2.5 %reshape_reshape.2 = bf16[32,48,512]{2,1,0:T(8,128)(2,1)S(1)} reshape(bf16[6,256,1,4,128]{4,3,1,0,2:T(4,128)(2,1)} %get-tuple-element.52) | data formatting | bytes 3145728 | tf_op jit(solution)/shard_map/reshape;reshape | solution.py:85
  49.8 1.3 convolution_convert_fusion
  51.1 0.9 copy.34
  52.0 56.0 %all_to_all.20 = bf16[32,48,512]{2,1,0:T(8,128)(2,1)S(1)} all-to-all(bf16[32,48,512]{2,1,0:T(8,128)(2,1)S(1)} %copy.34), channel_id=1, replica_groups=mesh['seq'=32,'head'=24] {'seq'}, dimensions={0} | all-to-all | bytes 3145728 | tf_op jit(solution)/shard_map/all_to_all | solution.py:92
  108.0 0.9 copy.35
  108.8 74.4 %all_to_all.21 = bf16[32,48,512]{2,0,1:T(8,128)(2,1)S(1)} all-to-all(bf16[32,48,512]{2,0,1:T(8,128)(2,1)S(1)} %copy.35), channel_id=1, replica_groups=mesh['seq'=32,'head'=24] {'head'}, dimensions={1} | all-to-all | bytes 3145728 | tf_op jit(solution)/shard_map/all_to_all | solution.py:91
  183.2 0.9 copy.36
  184.1 2.1 %broadcast_in_dim.16 = bf16[1,32,2,12288]{3,2,1,0:T(2,128)(2,1)} reshape(bf16[32,2,24,512]{3,2,1,0:T(8,128)(2,1)S(1)} %copy.36) | data formatting | bytes 3145728 | tf_op jit(solution)/shard_map/broadcast_in_dim | solution.py:98
  (35 shorter events, 0.5 us)
Async XLA Ops:
  0.0 12.2 %copy-start = (bf16[1536,128]{1,0:T(8,128)(2,1)S(1)}, bf16[1536,128]{1,0:T(8,128)(2,1)}, u32[]{:S(2)}) copy-start(bf16[1536,128]{1,0:T(8,128)(2,1)} %param.9) | copy-start | bytes 1179652
  0.0 12.1 %collective-permute-start = (bf16[1536,128]{1,0:T(8,128)(2,1)}, bf16[1536,128]{1,0:T(8,128)(2,1)S(1)}, u32[]{:S(2)}, u32[]{:S(2)}) collective-permute-start(bf16[1536,128]{1,0:T(8,128)(2,1)} %param.9), channel_id=1, source_target_pairs={{0,24},{24,48},{48,72},{72,96},{96,120},{120,144},{144,168},{168,1... | collective-permute-start | bytes 1179656 | tf_op jit(solution)/shard_map/ppermute | solution.py:17
  4.1 9.6 %collective-permute-start.1 = (bf16[1536,128]{1,0:T(8,128)(2,1)}, bf16[1536,128]{1,0:T(8,128)(2,1)}, u32[]{:S(2)}, u32[]{:S(2)}) collective-permute-start(bf16[1536,128]{1,0:T(8,128)(2,1)} %param.8), channel_id=1, source_target_pairs={{0,24},{24,48},{48,72},{72,96},{96,120},{120,144},{144,168},{168,1... | collective-permute-start | bytes 1179656 | tf_op jit(solution)/shard_map/ppermute | solution.py:17
  9.7 4.9 %copy-start.1 = (bf16[1536,128]{1,0:T(8,128)(2,1)S(1)}, bf16[1536,128]{1,0:T(8,128)(2,1)}, u32[]{:S(2)}) copy-start(bf16[1536,128]{1,0:T(8,128)(2,1)} %param.8) | copy-start | bytes 1179652
  47.3 2.5 %copy-start.2 = (s32[1,32]{1,0:T(1,128)S(1)}, s32[1,32]{1,0:T(1,128)}, u32[]{:S(2)}) copy-start(s32[1,32]{1,0:T(1,128)} %param.11) | copy-start | bytes 388
where the time goes:
time: 187 us; the launch traced here: 186 us
  blocking collectives  130 us (70%)
  local copies, waits for them, and re-layouts  17.2 us (9%)
  matrix products  17 us (9%)
  other arithmetic  11.7 us (6%)
  starting transfers between devices  7.92 us (4%)
    all_to_all x1, blocking collectives, per_device(): lax.all_to_all(lax.all_to_all(ordered, 'seq', split_axis=0, concat_axis=0...  74.4 us
    all_to_all x1, blocking collectives, per_device(): lax.all_to_all(ordered, 'seq', split_axis=0, concat_axis=0, tiled=True)  56 us
    dot_general x6, matrix products, attend_block(): jnp.einsum('hgqk,khd->qhgd', weights, v_window, preferred_element_type=jn...  11.8 us
    ppermute x2, starting transfers between devices, from_behind(): return lax.ppermute(block, axis, route)  7.92 us
    dynamic_update_slice x12, local copies, waits for them, and re-layouts, per_device(): lax.map(one_block, (q_blocks, k_blocks, v_blocks, qd_blocks, kd_blocks, q...  5.87 us
    and x6, other arithmetic, attend_block(): (k_doc[None, :] == q_doc[:, None]) & (k_pos[None, :] <= q_pos[:, None])  4.48 us
    reduce_sum x6, other arithmetic, attend_block(): weights = (expo / jnp.sum(expo, axis=3, keepdims=True)).astype(jnp.bfloat16)  4.1 us
    dot_general x6, matrix products, attend_block(): jnp.einsum('qhgd,khd->hgqk', q_block, k_window, preferred_element_type=jn...  3.83 us
  transfers between devices with their start and end apart: 2, of which 1 were waited for; matrix products, arithmetic and copies ran while one was open for 2% of the time, Pallas kernels for 0%

commit v1 on v0

--- a/solution.py
+++ b/solution.py
@@ -88,12 +88,13 @@
     ordered = jnp.einsum("op,prc->orc", one_hot, pieces, preferred_element_type=jnp.float32).astype(
         jnp.bfloat16
     )
-    arrived = lax.all_to_all(
-        lax.all_to_all(ordered, "seq", split_axis=0, concat_axis=0, tiled=True),
-        "head",
-        split_axis=1,
-        concat_axis=2,
-        tiled=True,
+    head_count = lax.axis_size("head")
+    rows_each = ordered.shape[1] // head_count
+    chunks = ordered.reshape(shard_count * head_count, rows_each, ordered.shape[2])
+    arrived = lax.all_to_all(chunks, ("seq", "head"), 0, 0, tiled=True)
+    arrived = arrived.reshape(shard_count, head_count, rows_each, ordered.shape[2])
+    arrived = jnp.transpose(arrived, (0, 2, 1, 3)).reshape(
+        shard_count, rows_each, head_count * ordered.shape[2]
     )
     return arrived[None]
 

time: 187 us -> 156 us (0.83)
  blocking collectives: 130 us -> 99.1 us
    all_to_all x2 -> x1, blocking collectives: 130 us -> 99.1 us  [per_device(): arrived = lax.all_to_all(chunks, ('seq', 'head'), 0, 0, tiled=True)]
    another operation x0 -> x2, local copies, waits for them, and re-layouts: none -> 3.53 us  [per_device(): return arrived[None]]
    broadcast_in_dim x1 -> x0, local copies, waits for them, and re-layouts: 2.05 us -> none  [per_device(): return arrived[None]]
  transfers between devices with their start and end apart: 2 -> 2, of which waited for: 1 -> 1; matrix products, arithmetic and copies ran while one was open for 2% -> 3% of each run, Pallas kernels for 0% -> 0%
where the time goes in v1:
time: 156 us
  blocking collectives  99.1 us (64%)
  local copies, waits for them, and re-layouts  17.9 us (11%)
  matrix products  17 us (11%)
  other arithmetic  11.7 us (8%)
  starting transfers between devices  7.92 us (5%)
    all_to_all x1, blocking collectives, per_device(): arrived = lax.all_to_all(chunks, ('seq', 'head'), 0, 0, tiled=True)  99.1 us
    dot_general x6, matrix products, attend_block(): jnp.einsum('hgqk,khd->qhgd', weights, v_window, preferred_element_type=jn...  11.8 us
    ppermute x2, starting transfers between devices, from_behind(): return lax.ppermute(block, axis, route)  7.92 us
    dynamic_update_slice x12, local copies, waits for them, and re-layouts, per_device(): lax.map(one_block, (q_blocks, k_blocks, v_blocks, qd_blocks, kd_blocks, q...  5.87 us
    and x6, other arithmetic, attend_block(): (k_doc[None, :] == q_doc[:, None]) & (k_pos[None, :] <= q_pos[:, None])  4.48 us
    reduce_sum x6, other arithmetic, attend_block(): weights = (expo / jnp.sum(expo, axis=3, keepdims=True)).astype(jnp.bfloat16)  4.1 us
    dot_general x6, matrix products, attend_block(): jnp.einsum('qhgd,khd->hgqk', q_block, k_window, preferred_element_type=jn...  3.83 us
    another operation x2, local copies, waits for them, and re-layouts, per_device(): return arrived[None]  3.53 us
  transfers between devices with their start and end apart: 2, of which 1 were waited for; matrix products, arithmetic and copies ran while one was open for 3% of the time, Pallas kernels for 0%

profile of v1, /device:TPU:1, one launch (start us, length us, event | category | flops | bytes accessed | tf_op | source)
XLA Modules:
  0.0 155.5 jit_solution(8330870418506572396)
XLA Ops:
  0.0 4.1 %collective-permute-start = (bf16[1536,128]{1,0:T(8,128)(2,1)}, bf16[1536,128]{1,0:T(8,128)(2,1)S(1)}, u32[]{:S(2)}, u32[]{:S(2)}) collective-permute-start(bf16[1536,128]{1,0:T(8,128)(2,1)} %param.9), channel_id=1, source_target_pairs={{0,24},{24,48},{48,72},{72,96},{96,120},{120,144},{144,168},{168,1... | collective-permute-start | bytes 1179656 | tf_op jit(solution)/shard_map/ppermute | solution.py:17
  4.1 3.8 %collective-permute-start.1 = (bf16[1536,128]{1,0:T(8,128)(2,1)}, bf16[1536,128]{1,0:T(8,128)(2,1)}, u32[]{:S(2)}, u32[]{:S(2)}) collective-permute-start(bf16[1536,128]{1,0:T(8,128)(2,1)} %param.8), channel_id=1, source_target_pairs={{0,24},{24,48},{48,72},{72,96},{96,120},{120,144},{144,168},{168,1... | collective-permute-start | bytes 1179656 | tf_op jit(solution)/shard_map/ppermute | solution.py:17
  7.9 0.8 multiply_reduce_fusion
  8.7 0.1 select_reduce_fusion
  8.9 0.7 convert_reduce_fusion
  9.7 0.0 copy-start.1
  9.7 2.4 %reshape.182 = bf16[6,256,1,4,128]{4,3,1,0,2:T(4,128)(2,1)S(1)} reshape(bf16[1536,512]{1,0:T(8,128)(2,1)} %param.7) | data formatting | bytes 3145728 | tf_op jit(solution)/shard_map/reshape | solution.py:69
  12.2 0.1 fusion.22
  12.2 1.5 collective-permute-done.1
  13.7 0.9 slice.130
  14.6 0.1 fusion.21
  14.7 1.1 pad_maximum_fusion
  15.8 0.1 pad_maximum_fusion.1
  15.9 31.4 %while.10 = (s32[]{:T(128)}, bf16[6,256,1,4,128]{4,3,1,0,2:T(4,128)(2,1)}, bf16[6,768,1,128]{3,1,0,2:T(8,128)(2,1)}, s32[6,768]{1,0:T(8,128)S(1)}, s32[6,256]{1,...) while((s32[]{:T(128)}, ...), condition=%wide.region_6.7_spmd, body=%wide.region_3.6_spmd.sunk | while | flops 413006592 | bytes 12764793 | solution.py:81
  16.0 0.7 and_and_fusion.2
  16.7 0.1 constant_dynamic-slice_fusion.7
  16.8 0.6 fusion.35
  17.5 0.7 fusion.36
  18.2 2.0 %fusion.37 = bf16[1,256,1,4,128]{1,4,3,2,0:T(8,128)(2,1)S(1)} fusion(f32[4,256]{1,0:T(4,128)S(1)} %fusion.36, f32[4,256]{1,0:T(4,128)S(1)} %get-tuple-element.173, f32[768,256,4]{1,0,2:T(8,128)S(1)} %get-tuple-element.172, pred[256,768]{0,1:T(8,128)(4,1)S(1)} %and_and_fusion.2, bf16[6,768,1,128]{3,1,0,2:T(8,128)(2,1)} %get-tuple-element.196, ...), kind=kOutput, calls=%fused_computation.8.clone.1 | convolution fusion | flops 205389824 | bytes 3809792 | tf_op jit(solution)/shard_map/while/body/eval_jaxpr/hgqk,khd->qhgd/dot_general | solution.py:33
  20.1 0.2 copy.37
  20.3 0.8 constant_dynamic-update-slice_fusion.2
  21.2 0.7 and_and_fusion.2
  22.0 0.1 constant_dynamic-slice_fusion.7
  22.1 0.6 fusion.35
  22.7 0.7 fusion.36
  23.4 2.0 %fusion.37 = bf16[1,256,1,4,128]{1,4,3,2,0:T(8,128)(2,1)S(1)} fusion(f32[4,256]{1,0:T(4,128)S(1)} %fusion.36, f32[4,256]{1,0:T(4,128)S(1)} %get-tuple-element.173, f32[768,256,4]{1,0,2:T(8,128)S(1)} %get-tuple-element.172, pred[256,768]{0,1:T(8,128)(4,1)S(1)} %and_and_fusion.2, bf16[6,768,1,128]{3,1,0,2:T(8,128)(2,1)} %get-tuple-element.196, ...), kind=kOutput, calls=%fused_computation.8.clone.1 | convolution fusion | flops 205389824 | bytes 3809792 | tf_op jit(solution)/shard_map/while/body/eval_jaxpr/hgqk,khd->qhgd/dot_general | solution.py:33
  25.4 0.2 copy.37
  25.6 0.8 constant_dynamic-update-slice_fusion.2
  26.4 0.7 and_and_fusion.2
  27.2 0.1 constant_dynamic-slice_fusion.7
  27.3 0.6 fusion.35
  27.9 0.7 fusion.36
  28.6 2.0 %fusion.37 = bf16[1,256,1,4,128]{1,4,3,2,0:T(8,128)(2,1)S(1)} fusion(f32[4,256]{1,0:T(4,128)S(1)} %fusion.36, f32[4,256]{1,0:T(4,128)S(1)} %get-tuple-element.173, f32[768,256,4]{1,0,2:T(8,128)S(1)} %get-tuple-element.172, pred[256,768]{0,1:T(8,128)(4,1)S(1)} %and_and_fusion.2, bf16[6,768,1,128]{3,1,0,2:T(8,128)(2,1)} %get-tuple-element.196, ...), kind=kOutput, calls=%fused_computation.8.clone.1 | convolution fusion | flops 205389824 | bytes 3809792 | tf_op jit(solution)/shard_map/while/body/eval_jaxpr/hgqk,khd->qhgd/dot_general | solution.py:33
  30.6 0.2 copy.37
  30.8 0.8 constant_dynamic-update-slice_fusion.2
  31.7 0.7 and_and_fusion.2
  32.4 0.1 constant_dynamic-slice_fusion.7
  32.5 0.6 fusion.35
  33.2 0.7 fusion.36
  33.9 2.0 %fusion.37 = bf16[1,256,1,4,128]{1,4,3,2,0:T(8,128)(2,1)S(1)} fusion(f32[4,256]{1,0:T(4,128)S(1)} %fusion.36, f32[4,256]{1,0:T(4,128)S(1)} %get-tuple-element.173, f32[768,256,4]{1,0,2:T(8,128)S(1)} %get-tuple-element.172, pred[256,768]{0,1:T(8,128)(4,1)S(1)} %and_and_fusion.2, bf16[6,768,1,128]{3,1,0,2:T(8,128)(2,1)} %get-tuple-element.196, ...), kind=kOutput, calls=%fused_computation.8.clone.1 | convolution fusion | flops 205389824 | bytes 3809792 | tf_op jit(solution)/shard_map/while/body/eval_jaxpr/hgqk,khd->qhgd/dot_general | solution.py:33
  35.8 0.2 copy.37
  36.0 0.8 constant_dynamic-update-slice_fusion.2
  36.9 0.7 and_and_fusion.2
  37.7 0.1 constant_dynamic-slice_fusion.7
  37.8 0.6 fusion.35
  38.4 0.7 fusion.36
  39.1 2.0 %fusion.37 = bf16[1,256,1,4,128]{1,4,3,2,0:T(8,128)(2,1)S(1)} fusion(f32[4,256]{1,0:T(4,128)S(1)} %fusion.36, f32[4,256]{1,0:T(4,128)S(1)} %get-tuple-element.173, f32[768,256,4]{1,0,2:T(8,128)S(1)} %get-tuple-element.172, pred[256,768]{0,1:T(8,128)(4,1)S(1)} %and_and_fusion.2, bf16[6,768,1,128]{3,1,0,2:T(8,128)(2,1)} %get-tuple-element.196, ...), kind=kOutput, calls=%fused_computation.8.clone.1 | convolution fusion | flops 205389824 | bytes 3809792 | tf_op jit(solution)/shard_map/while/body/eval_jaxpr/hgqk,khd->qhgd/dot_general | solution.py:33
  41.1 0.2 copy.37
  41.3 0.8 constant_dynamic-update-slice_fusion.2
  42.1 0.7 and_and_fusion.2
  42.9 0.1 constant_dynamic-slice_fusion.7
  43.0 0.6 fusion.35
  43.6 0.7 fusion.36
  44.3 2.0 %fusion.37 = bf16[1,256,1,4,128]{1,4,3,2,0:T(8,128)(2,1)S(1)} fusion(f32[4,256]{1,0:T(4,128)S(1)} %fusion.36, f32[4,256]{1,0:T(4,128)S(1)} %get-tuple-element.173, f32[768,256,4]{1,0,2:T(8,128)S(1)} %get-tuple-element.172, pred[256,768]{0,1:T(8,128)(4,1)S(1)} %and_and_fusion.2, bf16[6,768,1,128]{3,1,0,2:T(8,128)(2,1)} %get-tuple-element.196, ...), kind=kOutput, calls=%fused_computation.8.clone.1 | convolution fusion | flops 205389824 | bytes 3809792 | tf_op jit(solution)/shard_map/while/body/eval_jaxpr/hgqk,khd->qhgd/dot_general | solution.py:33
  46.3 0.2 copy.37
  46.5 0.8 constant_dynamic-update-slice_fusion.2
  47.3 2.5 %reshape_reshape.2 = bf16[32,48,512]{2,1,0:T(8,128)(2,1)S(1)} reshape(bf16[6,256,1,4,128]{4,3,1,0,2:T(4,128)(2,1)} %get-tuple-element.52) | data formatting | bytes 3145728 | tf_op jit(solution)/shard_map/reshape;reshape | solution.py:85
  49.8 1.3 convolution_convert_fusion
  51.1 0.9 copy.20
  52.0 0.6 reshape.183
  52.6 99.1 %all_to_all.5 = bf16[768,2,512]{2,1,0:T(2,128)(2,1)S(1)} all-to-all(bf16[768,2,512]{2,1,0:T(2,128)(2,1)S(1)} %reshape.183), channel_id=1, replica_groups=mesh['seq'=32,'head'=24] {'seq','head'}, dimensions={0} | all-to-all | bytes 3145728 | tf_op jit(solution)/shard_map/all_to_all | solution.py:94
  151.7 0.2 copy.21
  152.0 0.8 broadcast_in_dim_reshape.3
  152.7 2.8 %copy.22 = bf16[1,32,2,12288]{3,2,1,0:T(2,128)(2,1)} copy(bf16[1,32,2,12288]{3,1,2,0:T(8,128)(2,1)S(1)} %broadcast_in_dim_reshape.3) | data formatting | bytes 3145728 | tf_op jit(solution)/shard_map/broadcast_in_dim;reshape | solution.py:99
  (35 shorter events, 0.5 us)
Async XLA Ops:
  0.0 12.2 %copy-start = (bf16[1536,128]{1,0:T(8,128)(2,1)S(1)}, bf16[1536,128]{1,0:T(8,128)(2,1)}, u32[]{:S(2)}) copy-start(bf16[1536,128]{1,0:T(8,128)(2,1)} %param.9) | copy-start | bytes 1179652
  0.0 12.1 %collective-permute-start = (bf16[1536,128]{1,0:T(8,128)(2,1)}, bf16[1536,128]{1,0:T(8,128)(2,1)S(1)}, u32[]{:S(2)}, u32[]{:S(2)}) collective-permute-start(bf16[1536,128]{1,0:T(8,128)(2,1)} %param.9), channel_id=1, source_target_pairs={{0,24},{24,48},{48,72},{72,96},{96,120},{120,144},{144,168},{168,1... | collective-permute-start | bytes 1179656 | tf_op jit(solution)/shard_map/ppermute | solution.py:17
  4.1 9.6 %collective-permute-start.1 = (bf16[1536,128]{1,0:T(8,128)(2,1)}, bf16[1536,128]{1,0:T(8,128)(2,1)}, u32[]{:S(2)}, u32[]{:S(2)}) collective-permute-start(bf16[1536,128]{1,0:T(8,128)(2,1)} %param.8), channel_id=1, source_target_pairs={{0,24},{24,48},{48,72},{72,96},{96,120},{120,144},{144,168},{168,1... | collective-permute-start | bytes 1179656 | tf_op jit(solution)/shard_map/ppermute | solution.py:17
  9.7 4.9 %copy-start.1 = (bf16[1536,128]{1,0:T(8,128)(2,1)S(1)}, bf16[1536,128]{1,0:T(8,128)(2,1)}, u32[]{:S(2)}) copy-start(bf16[1536,128]{1,0:T(8,128)(2,1)} %param.8) | copy-start | bytes 1179652
  47.3 2.5 %copy-start.2 = (s32[1,32]{1,0:T(1,128)S(1)}, s32[1,32]{1,0:T(1,128)}, u32[]{:S(2)}) copy-start(s32[1,32]{1,0:T(1,128)} %param.11) | copy-start | bytes 388

commit v2 on v1

v2 whole, which is shorter than its diff:
```python
import functools
import math

import jax
import jax.numpy as jnp
from jax import lax
from jax.experimental import pallas as pl
from jax.sharding import PartitionSpec as P

HD = 128
KV_HEADS = 8
FILE_MOST = 512
QROWS = 256


def from_behind(block, axis, distance):
    devices = range(lax.axis_size(axis))
    route = [(i - distance, i) for i in devices if i - distance in devices]
    return lax.ppermute(block, axis, route)


def attend_kernel(q_ref, k_ref, v_ref, kd_ref, qd_ref, o_ref, *, scale, group):
    start = pl.multiple_of(pl.program_id(0) * QROWS, QROWS)
    k_window = k_ref[pl.ds(start, QROWS + FILE_MOST), :]
    v_window = v_ref[pl.ds(start, QROWS + FILE_MOST), :]
    row = lax.broadcasted_iota(jnp.int32, (QROWS, QROWS + FILE_MOST), 0)
    col = lax.broadcasted_iota(jnp.int32, (QROWS, QROWS + FILE_MOST), 1)
    allowed = (kd_ref[0] == qd_ref[...]) & (col <= row + FILE_MOST)
    for g in range(group):
        q_head = q_ref[:, g * HD : (g + 1) * HD]
        scores = (
            lax.dot_general(
                q_head, k_window, (((1,), (1,)), ((), ())), preferred_element_type=jnp.float32
            )
            * scale
        )
        scores = jnp.where(allowed, scores, -jnp.inf)
        row_max = jnp.max(scores, axis=1, keepdims=True)
        expo = jnp.exp(scores - row_max)
        weights = (expo / jnp.sum(expo, axis=1, keepdims=True)).astype(jnp.bfloat16)
        result = jnp.dot(weights, v_window, preferred_element_type=jnp.float32)
        o_ref[:, g * HD : (g + 1) * HD] = result.astype(o_ref.dtype)


def attend_local(queries, wide_keys, wide_values, kd_windows, q_doc, scale):
    tok_rows, width = queries.shape
    wide = wide_keys.shape[0]
    return pl.pallas_call(
        functools.partial(attend_kernel, scale=scale, group=width // HD),
        grid=(tok_rows // QROWS,),
        in_specs=[
            pl.BlockSpec((QROWS, width), lambda i: (i, 0)),
            pl.BlockSpec((wide, HD), lambda i: (0, 0)),
            pl.BlockSpec((wide, HD), lambda i: (0, 0)),
            pl.BlockSpec((1, 1, QROWS + FILE_MOST), lambda i: (i, 0, 0)),
            pl.BlockSpec((QROWS, 1), lambda i: (i, 0)),
        ],
        out_specs=pl.BlockSpec((QROWS, width), lambda i: (i, 0)),
        out_shape=jax.ShapeDtypeStruct((tok_rows, width), queries.dtype),
    )(queries, wide_keys, wide_values, kd_windows, q_doc)


def stacked_windows(array, block_count, reach):
    tiles = array.reshape((block_count + reach, QROWS) + array.shape[1:])
    return jnp.concatenate([tiles[step : step + block_count] for step in range(reach + 1)], axis=1)


def per_device(queries, keys, values, file_lengths, owner_of):
    tok_rows = queries.shape[0]
    heads_here = keys.shape[1] // HD
    shard_count = lax.axis_size("seq")
    head_count = lax.axis_size("head")
    offset = lax.axis_index("seq") * tok_rows
    sequence = lax.axis_index("head") * heads_here // KV_HEADS
    rim_keys, rim_values = from_behind(
        (keys[tok_rows - FILE_MOST :], values[tok_rows - FILE_MOST :]), "seq", 1
    )
    wide_keys = jnp.concatenate([rim_keys, keys], axis=0)
    wide_values = jnp.concatenate([rim_values, values], axis=0)
    file_count = file_lengths.shape[1]
    batch_pick = (jnp.arange(file_lengths.shape[0], dtype=jnp.int32) == sequence).astype(jnp.int32)
    lengths_here = jnp.sum(file_lengths * batch_pick[:, None], axis=0)
    file_index = jnp.arange(file_count, dtype=jnp.int32)
    upto = (file_index[:, None] <= file_index[None, :]).astype(jnp.int32)
    file_ends = jnp.sum(lengths_here[:, None] * upto, axis=0)
    positions = offset - FILE_MOST + jnp.arange(tok_rows + FILE_MOST, dtype=jnp.int32)
    doc_ids = jnp.sum((file_ends[None, :] <= positions[:, None]).astype(jnp.int32), axis=1)
    key_docs = jnp.where(positions >= 0, doc_ids, -1)
    scale = 1.0 / math.sqrt(HD)
    block_count = tok_rows // QROWS
    reach = FILE_MOST // QROWS
    kd_windows = stacked_windows(key_docs, block_count, reach).reshape(
        block_count, 1, QROWS + FILE_MOST
    )
    q_doc = doc_ids[FILE_MOST:].reshape(tok_rows, 1)
    if heads_here == 1:
        attended = attend_local(queries, wide_keys, wide_values, kd_windows, q_doc, scale)
    else:
        group_width = queries.shape[1] // heads_here
        attended = jnp.concatenate(
            [
                attend_local(
                    queries[:, h * group_width : (h + 1) * group_width],
                    wide_keys[:, h * HD : (h + 1) * HD],
                    wide_values[:, h * HD : (h + 1) * HD],
                    kd_windows,
                    q_doc,
                    scale,
                )
                for h in range(heads_here)
            ],
            axis=1,
        )
    pieces = attended.reshape(shard_count, tok_rows // shard_count, attended.shape[1])
    owner_index = jnp.arange(shard_count, dtype=jnp.int32)
    one_hot = (owner_of[0][None, :] == owner_index[:, None]).astype(jnp.bfloat16)
    ordered = jnp.einsum("op,prc->orc", one_hot, pieces, preferred_element_type=jnp.float32).astype(
        jnp.bfloat16
    )
    rows_each = ordered.shape[1] // head_count
    chunks = ordered.reshape(shard_count * head_count, rows_each, ordered.shape[2])
    arrived = lax.all_to_all(chunks, ("seq", "head"), 0, 0, tiled=True)
    arrived = arrived.reshape(shard_count, head_count, rows_each, ordered.shape[2])
    arrived = jnp.transpose(arrived, (0, 2, 1, 3)).reshape(
        shard_count, rows_each, head_count * ordered.shape[2]
    )
    return arrived[None]


def solution(mesh):
    return jax.shard_map(
        per_device,
        mesh=mesh,
        in_specs=(P("seq", "head"), P("seq", "head"), P("seq", "head"), P(), P("seq", None)),
        out_specs=P("seq", None, "head", None),
        check_vma=False,
    )
```

time: 156 us -> 130 us (0.83)
  Pallas kernels: 0 us -> 16.2 us
  matrix products: 17 us -> 2.69 us
  local copies, waits for them, and re-layouts: 17.9 us -> 8.98 us
  other arithmetic: 11.7 us -> 3.37 us
  blocking collectives: 99.1 us -> 90.8 us
    pallas_call x0 -> x1, Pallas kernels: none -> 16.2 us  [attend_local(): pl.pallas_call(functools.partial(attend_kernel, scale=scale, group=width...]
    dot_general x12 -> x0, matrix products: 15.7 us -> none  [the longest x6 11.8 us: attend_block(): jnp.einsum('hgqk,khd->qhgd', weights, v_window, preferred_element_type=jn...]
    all_to_all x1, blocking collectives: 99.1 us -> 90.8 us  [per_device(): arrived = lax.all_to_all(chunks, ('seq', 'head'), 0, 0, tiled=True)]
    dynamic_update_slice x12 -> x0, local copies, waits for them, and re-layouts: 5.87 us -> none  [per_device(): lax.map(one_block, (q_blocks, k_blocks, v_blocks, qd_blocks, kd_blocks, q...]
    and x6 -> x0, other arithmetic: 4.48 us -> none  [attend_block(): (k_doc[None, :] == q_doc[:, None]) & (k_pos[None, :] <= q_pos[:, None])]
    reduce_sum x6 -> x0, other arithmetic: 4.1 us -> none  [attend_block(): weights = (expo / jnp.sum(expo, axis=3, keepdims=True)).astype(jnp.bfloat16)]
    another operation x1 -> x0, local copies, waits for them, and re-layouts: 2.51 us -> none  [per_device(): attended.reshape(shard_count, tok_rows // shard_count, heads_here * group...]
    concatenate x2, other arithmetic: 0.11 us -> 1.7 us  [the longest x1 0.86 us: per_device(): wide_values = jnp.concatenate([rim_values, values], axis=0)]
  transfers between devices with their start and end apart: 2 -> 2, of which waited for: 1 -> 0; matrix products, arithmetic and copies ran while one was open for 3% -> 4% of each run, Pallas kernels for 0% -> 0%
where the time goes in v2:
time: 130 us; the launch traced here: 129 us
  blocking collectives  90.8 us (70%)
  Pallas kernels  16.2 us (12%)
  local copies, waits for them, and re-layouts  8.98 us (7%)
  starting transfers between devices  7.06 us (5%)
  other arithmetic  3.37 us (3%)
  matrix products  2.69 us (2%)
    all_to_all x1, blocking collectives, per_device(): arrived = lax.all_to_all(chunks, ('seq', 'head'), 0, 0, tiled=True)  90.8 us
    pallas_call x1, Pallas kernels, attend_local(): pl.pallas_call(functools.partial(attend_kernel, scale=scale, group=width...  16.2 us
    ppermute x2, starting transfers between devices, from_behind(): return lax.ppermute(block, axis, route)  7.06 us
    another operation x2, local copies, waits for them, and re-layouts, per_device(): return arrived[None]  3.53 us
    dot_general x1, matrix products, per_device(): jnp.einsum('op,prc->orc', one_hot, pieces, preferred_element_type=jnp.flo...  2.69 us
  transfers between devices with their start and end apart: 2, of which 0 were waited for; matrix products, arithmetic and copies ran while one was open for 4% of the time, Pallas kernels for 0%

profile of v2, /device:TPU:1, one launch (start us, length us, event | category | flops | bytes accessed | tf_op | source)
XLA Modules:
  0.0 129.3 jit_solution(11167073804186582816)
XLA Ops:
  0.0 0.0 copy-start.1
  0.0 0.0 copy-start
  0.0 1.0 slice.25
  1.0 3.9 %collective-permute-start.1 = (bf16[512,128]{1,0:T(8,128)(2,1)S(1)}, bf16[512,128]{1,0:T(8,128)(2,1)S(1)}, u32[]{:S(2)}, u32[]{:S(2)}) collective-permute-start(bf16[512,128]{1,0:T(8,128)(2,1)S(1)} %slice.25), channel_id=1, source_target_pairs={{0,24},{24,48},{48,72},{72,96},{96,120},{120,144},{144,168},{168,1... | collective-permute-start | bytes 393224 | tf_op jit(solution)/shard_map/ppermute | solution.py:19
  4.9 0.9 slice.24
  5.9 3.1 %collective-permute-start = (bf16[512,128]{1,0:T(8,128)(2,1)S(1)}, bf16[512,128]{1,0:T(8,128)(2,1)S(1)}, u32[]{:S(2)}, u32[]{:S(2)}) collective-permute-start(bf16[512,128]{1,0:T(8,128)(2,1)S(1)} %slice.24), channel_id=1, source_target_pairs={{0,24},{24,48},{48,72},{72,96},{96,120},{120,144},{144,168},{168,1... | collective-permute-start | bytes 393224 | tf_op jit(solution)/shard_map/ppermute | solution.py:19
  9.0 0.8 multiply_reduce_fusion
  9.8 0.1 select_reduce_fusion
  10.0 0.7 convert_reduce_fusion
  10.8 0.6 reshape.39.kd_ref
  11.4 1.1 reshape.45.qd_ref
  12.5 0.0 collective-permute-done
  12.5 0.0 copy-done
  12.5 0.8 pad_maximum_fusion.k_ref
  13.4 0.0 collective-permute-done.1
  13.4 0.0 copy-done.1
  13.4 0.9 pad_maximum_fusion.1.v_ref
  14.2 0.0 copy-start.2
  14.2 16.2 %shard_map.55 = bf16[1536,512]{1,0:T(8,128)(2,1)} custom-call(bf16[1536,512]{1,0:T(8,128)(2,1)} %q_ref.1, bf16[2048,128]{1,0:T(8,128)(2,1)} %pad_maximum_fusion.k_ref, bf16[2048,128]{1,0:T(8,128)(2,1)} %pad_maximum_fusion.1.v_ref, s32[6,1,768]{2,1,0:T(1,128)} %reshape.39.kd_ref, s32[1536,1]{1,0:T(8,128)} %reshape.45.qd_ref), custom_call_target="tpu_custom_call" | custom-call | tf_op jit(solution)/shard_map/pallas_call | solution.py:48
  30.5 0.0 copy-done.2
  30.5 2.7 %convolution_convert_fusion = bf16[32,48,512]{2,0,1:T(8,128)(2,1)S(1)} fusion(bf16[32,48,512]{2,1,0:T(8,128)(2,1)} %bitcast.13, s32[32]{0:T(128)S(1)} %bitcast.14), kind=kOutput, calls=%fused_computation.1 | convolution fusion | flops 51119104 | bytes 3145856 | tf_op jit(solution)/shard_map/op,prc->orc/dot_general | solution.py:117
  33.2 0.9 copy.14
  34.1 0.6 reshape.42
  34.7 90.8 %all_to_all.5 = bf16[768,2,512]{2,1,0:T(2,128)(2,1)S(1)} all-to-all(bf16[768,2,512]{2,1,0:T(2,128)(2,1)S(1)} %reshape.42), channel_id=1, replica_groups=mesh['seq'=32,'head'=24] {'seq','head'}, dimensions={0} | all-to-all | bytes 3145728 | tf_op jit(solution)/shard_map/all_to_all | solution.py:122
  125.5 0.2 copy.15
  125.8 0.8 broadcast_in_dim_reshape.3
  126.6 2.8 %copy.16 = bf16[1,32,2,12288]{3,2,1,0:T(2,128)(2,1)} copy(bf16[1,32,2,12288]{3,1,2,0:T(8,128)(2,1)S(1)} %broadcast_in_dim_reshape.3) | data formatting | bytes 3145728 | tf_op jit(solution)/shard_map/broadcast_in_dim;reshape | solution.py:127
  (7 shorter events, 0.0 us)
Async XLA Ops:
  0.0 13.4 %copy-start.1 = (bf16[1536,128]{1,0:T(8,128)(2,1)S(1)}, bf16[1536,128]{1,0:T(8,128)(2,1)}, u32[]{:S(2)}) copy-start(bf16[1536,128]{1,0:T(8,128)(2,1)} %param.7) | copy-start | bytes 1179652
  0.0 12.5 %copy-start = (bf16[1536,128]{1,0:T(8,128)(2,1)S(1)}, bf16[1536,128]{1,0:T(8,128)(2,1)}, u32[]{:S(2)}) copy-start(bf16[1536,128]{1,0:T(8,128)(2,1)} %param.6) | copy-start | bytes 1179652
  1.0 12.4 %collective-permute-start.1 = (bf16[512,128]{1,0:T(8,128)(2,1)S(1)}, bf16[512,128]{1,0:T(8,128)(2,1)S(1)}, u32[]{:S(2)}, u32[]{:S(2)}) collective-permute-start(bf16[512,128]{1,0:T(8,128)(2,1)S(1)} %slice.25), channel_id=1, source_target_pairs={{0,24},{24,48},{48,72},{72,96},{96,120},{120,144},{144,168},{168,1... | collective-permute-start | bytes 393224 | tf_op jit(solution)/shard_map/ppermute | solution.py:19
  5.9 6.7 %collective-permute-start = (bf16[512,128]{1,0:T(8,128)(2,1)S(1)}, bf16[512,128]{1,0:T(8,128)(2,1)S(1)}, u32[]{:S(2)}, u32[]{:S(2)}) collective-permute-start(bf16[512,128]{1,0:T(8,128)(2,1)S(1)} %slice.24), channel_id=1, source_target_pairs={{0,24},{24,48},{48,72},{72,96},{96,120},{120,144},{144,168},{168,1... | collective-permute-start | bytes 393224 | tf_op jit(solution)/shard_map/ppermute | solution.py:19
  14.2 16.3 %copy-start.2 = (s32[1,32]{1,0:T(1,128)S(1)}, s32[1,32]{1,0:T(1,128)}, u32[]{:S(2)}) copy-start(s32[1,32]{1,0:T(1,128)} %param.9) | copy-start | bytes 388

commit v3 on v2

v3 whole, which is shorter than its diff:
```python
import functools
import math

import jax
import jax.numpy as jnp
from jax import lax
from jax.experimental import pallas as pl
from jax.experimental.pallas import tpu as pltpu
from jax.sharding import PartitionSpec as P

HD = 128
KV_HEADS = 8
FILE_MOST = 512
QROWS = 256


def from_behind(block, axis, distance):
    devices = range(lax.axis_size(axis))
    route = [(i - distance, i) for i in devices if i - distance in devices]
    return lax.ppermute(block, axis, route)


def attend_kernel(owner_ref, offset_ref, q_ref, k_ref, v_ref, rk_ref, rv_ref, fe_row_ref, fe_col_ref,
                  o_ref, wide_k, wide_v, attended, *, scale, group, piece):
    step = pl.program_id(0)
    window = QROWS + FILE_MOST

    @pl.when(step == 0)
    def _():
        wide_k[0:FILE_MOST, :] = rk_ref[...]
        wide_k[FILE_MOST:, :] = k_ref[...]
        wide_v[0:FILE_MOST, :] = rv_ref[...]
        wide_v[FILE_MOST:, :] = v_ref[...]

    start = pl.multiple_of(step * QROWS, QROWS)
    k_window = wide_k[pl.ds(start, window), :]
    v_window = wide_v[pl.ds(start, window), :]
    first = offset_ref[0] + step * QROWS
    k_pos = first - FILE_MOST + lax.broadcasted_iota(jnp.int32, (1, window), 1)
    k_doc = jnp.sum((fe_col_ref[...] <= k_pos).astype(jnp.float32), axis=0, keepdims=True)
    k_doc = jnp.where(k_pos >= 0, k_doc, -1.0)
    q_pos = first + lax.broadcasted_iota(jnp.int32, (QROWS, 1), 0)
    q_doc = jnp.sum((fe_row_ref[...] <= q_pos).astype(jnp.float32), axis=1, keepdims=True)
    row = lax.broadcasted_iota(jnp.int32, (QROWS, window), 0)
    col = lax.broadcasted_iota(jnp.int32, (QROWS, window), 1)
    allowed = (k_doc == q_doc) & (col <= row + FILE_MOST)
    for g in range(group):
        q_head = q_ref[:, g * HD:(g + 1) * HD]
        scores = lax.dot_general(q_head, k_window, (((1,), (1,)), ((), ())),
                                 preferred_element_type=jnp.float32) * scale
        scores = jnp.where(allowed, scores, -jnp.inf)
        row_max = jnp.max(scores, axis=1, keepdims=True)
        expo = jnp.exp(scores - row_max)
        weights = (expo / jnp.sum(expo, axis=1, keepdims=True)).astype(jnp.bfloat16)
        result = jnp.dot(weights, v_window, preferred_element_type=jnp.float32)
        attended[pl.ds(start, QROWS), g * HD:(g + 1) * HD] = result.astype(attended.dtype)

    @pl.when(step == pl.num_programs(0) - 1)
    def _():
        for p in range(o_ref.shape[0]):
            o_ref[owner_ref[p]] = attended[p * piece:(p + 1) * piece, :]

def attend_ordered(owner_row, offset, queries, keys, values, rim_keys, rim_values, file_ends, scale):
    tok_rows, width = queries.shape
    shard_count = owner_row.shape[0]
    piece = tok_rows // shard_count
    fe_row = file_ends.reshape(1, -1)
    fe_col = file_ends.reshape(-1, 1)
    full = lambda shape: pl.BlockSpec(shape, lambda i, *_: (0,) * len(shape))
    grid_spec = pltpu.PrefetchScalarGridSpec(
        num_scalar_prefetch=2,
        grid=(tok_rows // QROWS,),
        in_specs=[
            pl.BlockSpec((QROWS, width), lambda i, *_: (i, 0)),
            full(keys.shape), full(values.shape), full(rim_keys.shape), full(rim_values.shape),
            full(fe_row.shape), full(fe_col.shape),
        ],
        out_specs=full((shard_count, piece, width)),
        scratch_shapes=[
            pltpu.VMEM((tok_rows + FILE_MOST, HD), keys.dtype),
            pltpu.VMEM((tok_rows + FILE_MOST, HD), values.dtype),
            pltpu.VMEM((tok_rows, width), queries.dtype),
        ],
    )
    return pl.pallas_call(
        functools.partial(attend_kernel, scale=scale, group=width // HD, piece=piece),
        grid_spec=grid_spec,
        out_shape=jax.ShapeDtypeStruct((shard_count, piece, width), queries.dtype),
        compiler_params=pltpu.CompilerParams(dimension_semantics=("arbitrary",)),
    )(owner_row, offset, queries, keys, values, rim_keys, rim_values, fe_row, fe_col)


def per_device(queries, keys, values, file_lengths, owner_of):
    tok_rows = queries.shape[0]
    heads_here = keys.shape[1] // HD
    shard_count = lax.axis_size("seq")
    head_count = lax.axis_size("head")
    offset = lax.axis_index("seq") * tok_rows
    sequence = lax.axis_index("head") * heads_here // KV_HEADS
    rim_keys, rim_values = from_behind(
        (keys[tok_rows - FILE_MOST :], values[tok_rows - FILE_MOST :]), "seq", 1
    )
    file_count = file_lengths.shape[1]
    batch_pick = (jnp.arange(file_lengths.shape[0], dtype=jnp.int32) == sequence).astype(jnp.int32)
    lengths_here = jnp.sum(file_lengths * batch_pick[:, None], axis=0)
    file_index = jnp.arange(file_count, dtype=jnp.int32)
    upto = (file_index[:, None] <= file_index[None, :]).astype(jnp.int32)
    file_ends = jnp.sum(lengths_here[:, None] * upto, axis=0)
    scale = 1.0 / math.sqrt(HD)
    ordered = attend_ordered(
        owner_of[0].astype(jnp.int32),
        jnp.reshape(offset, (1,)).astype(jnp.int32),
        queries,
        keys,
        values,
        rim_keys,
        rim_values,
        file_ends,
        scale,
    )
    rows_each = ordered.shape[1] // head_count
    chunks = ordered.reshape(shard_count * head_count, rows_each, ordered.shape[2])
    arrived = lax.all_to_all(chunks, ("seq", "head"), 0, 0, tiled=True)
    arrived = arrived.reshape(shard_count, head_count, rows_each, ordered.shape[2])
    arrived = jnp.transpose(arrived, (0, 2, 1, 3)).reshape(
        shard_count, rows_each, head_count * ordered.shape[2]
    )
    return arrived[None]


def solution(mesh):
    return jax.shard_map(
        per_device,
        mesh=mesh,
        in_specs=(P("seq", "head"), P("seq", "head"), P("seq", "head"), P(), P("seq", None)),
        out_specs=P("seq", None, "head", None),
        check_vma=False,
    )
```

time: 130 us -> 127 us (0.977)
  matrix products: 2.69 us -> 0 us
  other arithmetic: 3.37 us -> 0.91 us
    dot_general x1 -> x0, matrix products: 2.69 us -> none  [per_device(): jnp.einsum('op,prc->orc', one_hot, pieces, preferred_element_type=jnp.flo...]
    reshape x1, local copies, waits for them, and re-layouts: 0.65 us -> 2.5 us  [per_device(): ordered.reshape(shard_count * head_count, rows_each, ordered.shape[2])]
    concatenate x3 -> x0, other arithmetic: 1.7 us -> none  [the longest x1 0.86 us: per_device(): wide_values = jnp.concatenate([rim_values, values], axis=0)]
    another operation x2 -> x1, local copies, waits for them, and re-layouts: 3.53 us -> 2.05 us  [per_device(): return arrived[None]]
  transfers between devices with their start and end apart: 2 -> 2, of which waited for: 0 -> 0; matrix products, arithmetic and copies ran while one was open for 4% -> 3% of each run, Pallas kernels for 0% -> 0%
where the time goes in v3:
time: 127 us; the launch traced here: 126 us
  blocking collectives  92 us (72%)
  Pallas kernels  17.4 us (14%)
  local copies, waits for them, and re-layouts  8.79 us (7%)
  starting transfers between devices  7.06 us (6%)
    all_to_all x1, blocking collectives, per_device(): arrived = lax.all_to_all(chunks, ('seq', 'head'), 0, 0, tiled=True)  92 us
    pallas_call x1, Pallas kernels, attend_ordered(): pl.pallas_call(functools.partial(attend_kernel, scale=scale, group=width...  17.4 us
    ppermute x2, starting transfers between devices, from_behind(): return lax.ppermute(block, axis, route)  7.06 us
  transfers between devices with their start and end apart: 2, of which 0 were waited for; matrix products, arithmetic and copies ran while one was open for 3% of the time, Pallas kernels for 0%

profile of v3, /device:TPU:1, one launch (start us, length us, event | category | flops | bytes accessed | tf_op | source)
XLA Modules:
  0.0 126.2 jit_solution(17271567073985406719)
XLA Ops:
  0.0 0.9 slice.7
  0.9 3.9 %collective-permute-start.1 = (bf16[512,128]{1,0:T(8,128)(2,1)S(1)}, bf16[512,128]{1,0:T(8,128)(2,1)S(1)}, u32[]{:S(2)}, u32[]{:S(2)}) collective-permute-start(bf16[512,128]{1,0:T(8,128)(2,1)S(1)} %slice.7), channel_id=1, source_target_pairs={{0,24},{24,48},{48,72},{72,96},{96,120},{120,144},{144,168},{168,1... | collective-permute-start | bytes 393224 | tf_op jit(solution)/shard_map/ppermute | solution.py:20
  4.9 0.9 slice.6
  5.8 3.1 %collective-permute-start = (bf16[512,128]{1,0:T(8,128)(2,1)S(1)}, bf16[512,128]{1,0:T(8,128)(2,1)S(1)}, u32[]{:S(2)}, u32[]{:S(2)}) collective-permute-start(bf16[512,128]{1,0:T(8,128)(2,1)S(1)} %slice.6), channel_id=1, source_target_pairs={{0,24},{24,48},{48,72},{72,96},{96,120},{120,144},{144,168},{168,1... | collective-permute-start | bytes 393224 | tf_op jit(solution)/shard_map/ppermute | solution.py:20
  9.0 0.8 multiply_reduce_fusion
  9.7 0.1 select_reduce_fusion
  9.9 0.6 reshape.22.fe_row_ref
  10.5 0.8 reshape.26.fe_col_ref
  11.2 0.0 collective-permute-done.1.rv_ref
  11.2 0.0 copy-start
  11.3 0.0 collective-permute-done.rk_ref
  11.3 0.0 copy-start.1
  11.3 0.6 copy-done
  11.9 0.1 copy-done.1
  12.0 17.4 %shard_map.55 = bf16[32,48,512]{2,1,0:T(8,128)(2,1)} custom-call(s32[32]{0:T(128)} %bitcast.10, s32[1]{0:T(128)} %bitcast.1.offset_ref, bf16[1536,512]{1,0:T(8,128)(2,1)} %q_ref.1, bf16[1536,128]{1,0:T(8,128)(2,1)} %k_ref.1, bf16[1536,128]{1,0:T(8,128)(2,1)} %v_ref.1, bf16[512,128]{1,0:T(8,128)(2,1)} %copy-done.1, bf16[512,128]{1,0:T(8,128)(2,1)} %copy-done, ...), custom_call_target="tpu_custom_call" | custom-call | tf_op jit(solution)/shard_map/pallas_call | solution.py:85
  29.4 2.5 %reshape.24 = bf16[768,2,512]{2,1,0:T(2,128)(2,1)S(1)} reshape(bf16[32,48,512]{2,1,0:T(8,128)(2,1)} %shard_map.55) | data formatting | bytes 3145728 | tf_op jit(solution)/shard_map/reshape | solution.py:122
  31.9 92.0 %all_to_all.5 = bf16[768,2,512]{2,1,0:T(2,128)(2,1)S(1)} all-to-all(bf16[768,2,512]{2,1,0:T(2,128)(2,1)S(1)} %reshape.24), channel_id=1, replica_groups=mesh['seq'=32,'head'=24] {'seq','head'}, dimensions={0} | all-to-all | bytes 3145728 | tf_op jit(solution)/shard_map/all_to_all | solution.py:123
  123.8 0.3 copy.12
  124.2 2.1 %broadcast_in_dim_reshape.3 = bf16[1,32,2,12288]{3,2,1,0:T(2,128)(2,1)} reshape(bf16[32,2,24,512]{3,2,1,0:T(8,128)(2,1)S(1)} %bitcast.9) | data formatting | bytes 3145728 | tf_op jit(solution)/shard_map/broadcast_in_dim;reshape | solution.py:128
  (1 shorter events, 0.0 us)
Async XLA Ops:
  0.9 10.3 %collective-permute-start.1 = (bf16[512,128]{1,0:T(8,128)(2,1)S(1)}, bf16[512,128]{1,0:T(8,128)(2,1)S(1)}, u32[]{:S(2)}, u32[]{:S(2)}) collective-permute-start(bf16[512,128]{1,0:T(8,128)(2,1)S(1)} %slice.7), channel_id=1, source_target_pairs={{0,24},{24,48},{48,72},{72,96},{96,120},{120,144},{144,168},{168,1... | collective-permute-start | bytes 393224 | tf_op jit(solution)/shard_map/ppermute | solution.py:20
  5.8 5.5 %collective-permute-start = (bf16[512,128]{1,0:T(8,128)(2,1)S(1)}, bf16[512,128]{1,0:T(8,128)(2,1)S(1)}, u32[]{:S(2)}, u32[]{:S(2)}) collective-permute-start(bf16[512,128]{1,0:T(8,128)(2,1)S(1)} %slice.6), channel_id=1, source_target_pairs={{0,24},{24,48},{48,72},{72,96},{96,120},{120,144},{144,168},{168,1... | collective-permute-start | bytes 393224 | tf_op jit(solution)/shard_map/ppermute | solution.py:20
  11.2 0.7 copy-start
  11.3 0.7 copy-start.1

commit v4 on v3

v4 whole, which is shorter than its diff:
```python
import functools
import math

import jax
import jax.numpy as jnp
from jax import lax
from jax.experimental import pallas as pl
from jax.experimental.pallas import tpu as pltpu
from jax.sharding import PartitionSpec as P

HD = 128
KV_HEADS = 8
FILE_MOST = 512
QROWS = 256
TRIM = 128
TRIMS = 2


def from_behind(block, axis, distance):
    devices = range(lax.axis_size(axis))
    route = [(i - distance, i) for i in devices if i - distance in devices]
    return lax.ppermute(block, axis, route)


def attend_kernel(owner_ref, offset_ref, trim_ref, q_ref, k_ref, v_ref, rim_ref, fe_row_ref, fe_col_ref,
                  o_ref, wide_k, wide_v, attended, *, scale, group, piece):
    step = pl.program_id(0)

    @pl.when(step == 0)
    def _():
        wide_k[0:FILE_MOST, :] = rim_ref[:, 0:HD]
        wide_k[FILE_MOST:, :] = k_ref[...]
        wide_v[0:FILE_MOST, :] = rim_ref[:, HD:2 * HD]
        wide_v[FILE_MOST:, :] = v_ref[...]

    start = pl.multiple_of(step * QROWS, QROWS)
    first = offset_ref[0] + step * QROWS
    q_pos = first + lax.broadcasted_iota(jnp.int32, (QROWS, 1), 0)
    q_doc = jnp.sum((fe_row_ref[...] <= q_pos).astype(jnp.float32), axis=1, keepdims=True)

    def attend(lo):
        window = QROWS + FILE_MOST - lo
        k_window = wide_k[pl.ds(pl.multiple_of(start + lo, TRIM), window), :]
        v_window = wide_v[pl.ds(pl.multiple_of(start + lo, TRIM), window), :]
        k_pos = first - FILE_MOST + lo + lax.broadcasted_iota(jnp.int32, (1, window), 1)
        k_doc = jnp.sum((fe_col_ref[...] <= k_pos).astype(jnp.float32), axis=0, keepdims=True)
        k_doc = jnp.where(k_pos >= 0, k_doc, -1.0)
        row = lax.broadcasted_iota(jnp.int32, (QROWS, window), 0)
        col = lax.broadcasted_iota(jnp.int32, (QROWS, window), 1)
        allowed = (k_doc == q_doc) & (col + lo <= row + FILE_MOST)
        for g in range(group):
            q_head = q_ref[:, g * HD:(g + 1) * HD]
            scores = lax.dot_general(q_head, k_window, (((1,), (1,)), ((), ())),
                                     preferred_element_type=jnp.float32) * scale
            scores = jnp.where(allowed, scores, -jnp.inf)
            row_max = jnp.max(scores, axis=1, keepdims=True)
            expo = jnp.exp(scores - row_max)
            weights = (expo / jnp.sum(expo, axis=1, keepdims=True)).astype(jnp.bfloat16)
            result = jnp.dot(weights, v_window, preferred_element_type=jnp.float32)
            attended[pl.ds(start, QROWS), g * HD:(g + 1) * HD] = result.astype(attended.dtype)

    for t in range(TRIMS + 1):
        pl.when(trim_ref[step] == t)(functools.partial(attend, t * TRIM))

    @pl.when(step == pl.num_programs(0) - 1)
    def _():
        for p in range(o_ref.shape[0]):
            o_ref[owner_ref[p]] = attended[p * piece:(p + 1) * piece, :]

def leading_trims(offset, file_ends, block_count):
    firsts = offset + QROWS * jnp.arange(block_count, dtype=jnp.int32)
    starts = jnp.max(jnp.where(file_ends[None, :] <= firsts[:, None], file_ends[None, :], 0), axis=1)
    lasts = firsts[:, None] - FILE_MOST + TRIM - 1 + TRIM * jnp.arange(TRIMS, dtype=jnp.int32)[None, :]
    return jnp.sum((lasts < starts[:, None]).astype(jnp.int32), axis=1)

def attend_ordered(owner_row, offset, queries, keys, values, rim, file_ends, scale):
    tok_rows, width = queries.shape
    shard_count = owner_row.shape[0]
    piece = tok_rows // shard_count
    block_count = tok_rows // QROWS
    trims = leading_trims(offset, file_ends, block_count)
    fe_row = file_ends.reshape(1, -1)
    fe_col = file_ends.reshape(-1, 1)
    full = lambda shape: pl.BlockSpec(shape, lambda i, *_: (0,) * len(shape))
    grid_spec = pltpu.PrefetchScalarGridSpec(
        num_scalar_prefetch=3,
        grid=(block_count,),
        in_specs=[
            pl.BlockSpec((QROWS, width), lambda i, *_: (i, 0)),
            full(keys.shape), full(values.shape), full(rim.shape),
            full(fe_row.shape), full(fe_col.shape),
        ],
        out_specs=full((shard_count, piece, width)),
        scratch_shapes=[
            pltpu.VMEM((tok_rows + FILE_MOST, HD), keys.dtype),
            pltpu.VMEM((tok_rows + FILE_MOST, HD), values.dtype),
            pltpu.VMEM((tok_rows, width), queries.dtype),
        ],
    )
    return pl.pallas_call(
        functools.partial(attend_kernel, scale=scale, group=width // HD, piece=piece),
        grid_spec=grid_spec,
        out_shape=jax.ShapeDtypeStruct((shard_count, piece, width), queries.dtype),
        compiler_params=pltpu.CompilerParams(dimension_semantics=("arbitrary",)),
    )(owner_row, jnp.reshape(offset, (1,)), trims, queries, keys, values, rim, fe_row, fe_col)


def per_device(queries, keys, values, file_lengths, owner_of):
    tok_rows = queries.shape[0]
    heads_here = keys.shape[1] // HD
    shard_count = lax.axis_size("seq")
    head_count = lax.axis_size("head")
    offset = lax.axis_index("seq") * tok_rows
    sequence = lax.axis_index("head") * heads_here // KV_HEADS
    rim = from_behind(
        jnp.concatenate([keys[tok_rows - FILE_MOST :], values[tok_rows - FILE_MOST :]], axis=1),
        "seq",
        1,
    )
    file_count = file_lengths.shape[1]
    batch_pick = (jnp.arange(file_lengths.shape[0], dtype=jnp.int32) == sequence).astype(jnp.int32)
    lengths_here = jnp.sum(file_lengths * batch_pick[:, None], axis=0)
    file_index = jnp.arange(file_count, dtype=jnp.int32)
    upto = (file_index[:, None] <= file_index[None, :]).astype(jnp.int32)
    file_ends = jnp.sum(lengths_here[:, None] * upto, axis=0)
    scale = 1.0 / math.sqrt(HD)
    ordered = attend_ordered(
        owner_of[0].astype(jnp.int32),
        offset.astype(jnp.int32),
        queries,
        keys,
        values,
        rim,
        file_ends,
        scale,
    )
    rows_each = ordered.shape[1] // head_count
    chunks = ordered.reshape(shard_count * head_count, rows_each, ordered.shape[2])
    arrived = lax.all_to_all(chunks, ("seq", "head"), 0, 0, tiled=True)
    arrived = arrived.reshape(shard_count, head_count, rows_each, ordered.shape[2])
    arrived = jnp.transpose(arrived, (0, 2, 1, 3)).reshape(
        shard_count, rows_each, head_count * ordered.shape[2]
    )
    return arrived[None]


def solution(mesh):
    return jax.shard_map(
        per_device,
        mesh=mesh,
        in_specs=(P("seq", "head"), P("seq", "head"), P("seq", "head"), P(), P("seq", None)),
        out_specs=P("seq", None, "head", None),
        check_vma=False,
    )
```

time: 127 us -> 124 us (0.976)
  starting transfers between devices: 7.06 us -> 3.95 us
    ppermute x2 -> x1, starting transfers between devices: 7.06 us -> 3.95 us  [from_behind(): return lax.ppermute(block, axis, route)]
  transfers between devices with their start and end apart: 2 -> 1, of which waited for: 0 -> 1; matrix products, arithmetic and copies ran while one was open for 3% -> 3% of each run, Pallas kernels for 0% -> 0%
where the time goes in v4:
time: 124 us
  blocking collectives  93.2 us (75%)
  Pallas kernels  16.2 us (13%)
  local copies, waits for them, and re-layouts  8.79 us (7%)
  starting transfers between devices  3.95 us (3%)
  other arithmetic  1.76 us (1%)
    all_to_all x1, blocking collectives, per_device(): arrived = lax.all_to_all(chunks, ('seq', 'head'), 0, 0, tiled=True)  93.2 us
    pallas_call x1, Pallas kernels, attend_ordered(): pl.pallas_call(functools.partial(attend_kernel, scale=scale, group=width...  16.2 us
    ppermute x1, starting transfers between devices, from_behind(): return lax.ppermute(block, axis, route)  3.95 us
    reshape x1, local copies, waits for them, and re-layouts, per_device(): ordered.reshape(shard_count * head_count, rows_each, ordered.shape[2])  2.5 us
  transfers between devices with their start and end apart: 1, of which 1 were waited for; matrix products, arithmetic and copies ran while one was open for 3% of the time, Pallas kernels for 0%

profile of v4, /device:TPU:1, one launch (start us, length us, event | category | flops | bytes accessed | tf_op | source)
XLA Modules:
  0.0 124.1 jit_solution(2951114404973383294)
XLA Ops:
  0.0 0.9 slice.6
  0.9 0.9 slice.7
  1.9 3.9 %collective-permute-start = (bf16[512,256]{1,0:T(8,128)(2,1)S(1)}, bf16[512,256]{1,0:T(8,128)(2,1)S(1)}, u32[]{:S(2)}, u32[]{:S(2)}) collective-permute-start(bf16[512,256]{1,0:T(8,128)(2,1)S(1)} %pad_maximum_fusion), channel_id=1, source_target_pairs={{0,24},{24,48},{48,72},{72,96},{96,120},{120,144},{144,168},{168,1... | collective-permute-start | bytes 786440 | tf_op jit(solution)/shard_map/ppermute | solution.py:22
  5.9 0.8 multiply_reduce_fusion
  6.7 0.1 select_reduce_fusion
  6.8 0.6 broadcast_in_dim.9.fe_row_ref
  7.4 0.8 reshape.42.fe_col_ref
  8.2 0.2 select_reduce_fusion.1
  8.4 0.6 fusion.trim_ref
  9.0 0.1 collective-permute-done.rim_ref
  9.1 0.0 copy-start
  9.1 0.7 copy-done
  9.8 16.2 %shard_map.55 = bf16[32,48,512]{2,1,0:T(8,128)(2,1)} custom-call(s32[32]{0:T(128)} %bitcast.10, s32[1]{0:T(128)} %bitcast.1.offset_ref, s32[6]{0:T(128)} %fusion.trim_ref, bf16[1536,512]{1,0:T(8,128)(2,1)} %q_ref.1, bf16[1536,128]{1,0:T(8,128)(2,1)} %k_ref.1, bf16[1536,128]{1,0:T(8,128)(2,1)} %v_ref.1, bf16[512,256]{1,0:T(8,128)(2,1)} %copy-done, ...), custom_call_target="tpu_custom_call" | custom-call | tf_op jit(solution)/shard_map/pallas_call | solution.py:100
  26.0 2.5 %reshape.40 = bf16[768,2,512]{2,1,0:T(2,128)(2,1)S(1)} reshape(bf16[32,48,512]{2,1,0:T(8,128)(2,1)} %shard_map.55) | data formatting | bytes 3145728 | tf_op jit(solution)/shard_map/reshape | solution.py:138
  28.6 93.2 %all_to_all.5 = bf16[768,2,512]{2,1,0:T(2,128)(2,1)S(1)} all-to-all(bf16[768,2,512]{2,1,0:T(2,128)(2,1)S(1)} %reshape.40), channel_id=1, replica_groups=mesh['seq'=32,'head'=24] {'seq','head'}, dimensions={0} | all-to-all | bytes 3145728 | tf_op jit(solution)/shard_map/all_to_all | solution.py:139
  121.7 0.3 copy.12
  122.1 2.1 %broadcast_in_dim_reshape.3 = bf16[1,32,2,12288]{3,2,1,0:T(2,128)(2,1)} reshape(bf16[32,2,24,512]{3,2,1,0:T(8,128)(2,1)S(1)} %bitcast.9) | data formatting | bytes 3145728 | tf_op jit(solution)/shard_map/broadcast_in_dim;reshape | solution.py:144
  (5 shorter events, 0.0 us)
Async XLA Ops:
  1.9 7.2 %collective-permute-start = (bf16[512,256]{1,0:T(8,128)(2,1)S(1)}, bf16[512,256]{1,0:T(8,128)(2,1)S(1)}, u32[]{:S(2)}, u32[]{:S(2)}) collective-permute-start(bf16[512,256]{1,0:T(8,128)(2,1)S(1)} %pad_maximum_fusion), channel_id=1, source_target_pairs={{0,24},{24,48},{48,72},{72,96},{96,120},{120,144},{144,168},{168,1... | collective-permute-start | bytes 786440 | tf_op jit(solution)/shard_map/ppermute | solution.py:22
  9.1 0.7 copy-start

commit v5 on v4

--- a/solution.py
+++ b/solution.py
@@ -105,6 +105,32 @@
     )(owner_row, jnp.reshape(offset, (1,)), trims, queries, keys, values, rim, fe_row, fe_col)
 
 
+def place_kernel(src_ref, dst_ref, sems):
+    heads = src_ref.shape[1]
+    width = src_ref.shape[3]
+    copies = [
+        pltpu.make_async_copy(
+            src_ref.at[:, h], dst_ref.at[:, :, pl.ds(h * width, width)], sems.at[h]
+        )
+        for h in range(heads)
+    ]
+    for copy in copies:
+        copy.start()
+    for copy in copies:
+        copy.wait()
+
+
+def place_rows(arrived):
+    shard_count, heads, rows, width = arrived.shape
+    return pl.pallas_call(
+        place_kernel,
+        in_specs=[pl.BlockSpec(memory_space=pl.ANY)],
+        out_specs=pl.BlockSpec(memory_space=pl.ANY),
+        out_shape=jax.ShapeDtypeStruct((shard_count, rows, heads * width), arrived.dtype),
+        scratch_shapes=[pltpu.SemaphoreType.DMA((heads,))],
+    )(arrived)
+
+
 def per_device(queries, keys, values, file_lengths, owner_of):
     tok_rows = queries.shape[0]
     heads_here = keys.shape[1] // HD
@@ -138,10 +164,7 @@
     chunks = ordered.reshape(shard_count * head_count, rows_each, ordered.shape[2])
     arrived = lax.all_to_all(chunks, ("seq", "head"), 0, 0, tiled=True)
     arrived = arrived.reshape(shard_count, head_count, rows_each, ordered.shape[2])
-    arrived = jnp.transpose(arrived, (0, 2, 1, 3)).reshape(
-        shard_count, rows_each, head_count * ordered.shape[2]
-    )
-    return arrived[None]
+    return place_rows(arrived)[None]
 
 
 def solution(mesh):

time: 124 us -> 172 us (1.39)
  Pallas kernels: 16.2 us -> 64.8 us
  local copies, waits for them, and re-layouts: 8.79 us -> 6.4 us
    pallas_call x0 -> x1, Pallas kernels: none -> 49 us  [place_rows(): pl.pallas_call(place_kernel, in_specs=[pl.BlockSpec(memory_space=pl.ANY)]...]
    another operation x1 -> x0, local copies, waits for them, and re-layouts: 2.05 us -> none  [per_device(): return arrived[None]]
  transfers between devices with their start and end apart: 1 -> 1, of which waited for: 1 -> 1; matrix products, arithmetic and copies ran while one was open for 3% -> 2% of each run, Pallas kernels for 0% -> 0%
where the time goes in v5:
time: 172 us; the launch traced here: 171 us
  blocking collectives  94.2 us (55%)
  Pallas kernels  64.8 us (38%)
  local copies, waits for them, and re-layouts  6.4 us (4%)
  starting transfers between devices  3.95 us (2%)
  other arithmetic  1.76 us (1%)
    all_to_all x1, blocking collectives, per_device(): arrived = lax.all_to_all(chunks, ('seq', 'head'), 0, 0, tiled=True)  94.2 us
    pallas_call x1, Pallas kernels, place_rows(): pl.pallas_call(place_kernel, in_specs=[pl.BlockSpec(memory_space=pl.ANY)]...  49 us
    pallas_call x1, Pallas kernels, attend_ordered(): pl.pallas_call(functools.partial(attend_kernel, scale=scale, group=width...  15.8 us
    ppermute x1, starting transfers between devices, from_behind(): return lax.ppermute(block, axis, route)  3.95 us
  transfers between devices with their start and end apart: 1, of which 1 were waited for; matrix products, arithmetic and copies ran while one was open for 2% of the time, Pallas kernels for 0%

profile of v5, /device:TPU:1, one launch (start us, length us, event | category | flops | bytes accessed | tf_op | source)
XLA Modules:
  0.0 171.2 jit_solution(1037897696107321729)
XLA Ops:
  0.0 0.9 slice.6
  0.9 0.9 slice.7
  1.9 3.9 %collective-permute-start = (bf16[512,256]{1,0:T(8,128)(2,1)S(1)}, bf16[512,256]{1,0:T(8,128)(2,1)S(1)}, u32[]{:S(2)}, u32[]{:S(2)}) collective-permute-start(bf16[512,256]{1,0:T(8,128)(2,1)S(1)} %pad_maximum_fusion), channel_id=1, source_target_pairs={{0,24},{24,48},{48,72},{72,96},{96,120},{120,144},{144,168},{168,1... | collective-permute-start | bytes 786440 | tf_op jit(solution)/shard_map/ppermute | solution.py:22
  5.9 0.8 multiply_reduce_fusion
  6.7 0.1 select_reduce_fusion
  6.8 0.6 broadcast_in_dim.15.fe_row_ref
  7.4 0.8 reshape.42.fe_col_ref
  8.2 0.2 select_reduce_fusion.1
  8.4 0.6 fusion.trim_ref
  9.0 0.1 collective-permute-done.rim_ref
  9.1 0.0 copy-start
  9.1 0.7 copy-done
  9.8 15.8 %shard_map.55 = bf16[32,48,512]{2,1,0:T(8,128)(2,1)} custom-call(s32[32]{0:T(128)} %bitcast.5, s32[1]{0:T(128)} %bitcast.1.offset_ref, s32[6]{0:T(128)} %fusion.trim_ref, bf16[1536,512]{1,0:T(8,128)(2,1)} %q_ref.1, bf16[1536,128]{1,0:T(8,128)(2,1)} %k_ref.1, bf16[1536,128]{1,0:T(8,128)(2,1)} %v_ref.1, bf16[512,256]{1,0:T(8,128)(2,1)} %copy-done, ...), custom_call_target="tpu_custom_call" | custom-call | tf_op jit(solution)/shard_map/pallas_call | solution.py:100
  25.6 2.5 %reshape.40 = bf16[768,2,512]{2,1,0:T(2,128)(2,1)S(1)} reshape(bf16[32,48,512]{2,1,0:T(8,128)(2,1)} %shard_map.55) | data formatting | bytes 3145728 | tf_op jit(solution)/shard_map/reshape | solution.py:164
  28.1 94.2 %all_to_all.5 = bf16[768,2,512]{2,1,0:T(2,128)(2,1)} all-to-all(bf16[768,2,512]{2,1,0:T(2,128)(2,1)S(1)} %reshape.40), channel_id=1, replica_groups=mesh['seq'=32,'head'=24] {'seq','head'}, dimensions={0} | all-to-all | bytes 3145728 | tf_op jit(solution)/shard_map/all_to_all | solution.py:165
  122.3 49.0 %shard_map.56 = bf16[32,2,12288]{2,1,0:T(2,128)(2,1)} custom-call(bf16[32,24,2,512]{3,2,1,0:T(2,128)(2,1)} %bitcast.4), custom_call_target="tpu_custom_call" | custom-call | tf_op jit(solution)/shard_map/pallas_call | solution.py:125
  (5 shorter events, 0.0 us)
Async XLA Ops:
  1.9 7.2 %collective-permute-start = (bf16[512,256]{1,0:T(8,128)(2,1)S(1)}, bf16[512,256]{1,0:T(8,128)(2,1)S(1)}, u32[]{:S(2)}, u32[]{:S(2)}) collective-permute-start(bf16[512,256]{1,0:T(8,128)(2,1)S(1)} %pad_maximum_fusion), channel_id=1, source_target_pairs={{0,24},{24,48},{48,72},{72,96},{96,120},{120,144},{144,168},{168,1... | collective-permute-start | bytes 786440 | tf_op jit(solution)/shard_map/ppermute | solution.py:22
  9.1 0.7 copy-start

commit v6 on v4

v6 whole, which is shorter than its diff:
```python
import functools
import math

import jax
import jax.numpy as jnp
from jax import lax
from jax.experimental import pallas as pl
from jax.experimental.pallas import tpu as pltpu
from jax.sharding import PartitionSpec as P

HD = 128
KV_HEADS = 8
FILE_MOST = 512
QROWS = 256
TRIM = 128
TRIMS = 2


def from_behind(block, axis, distance):
    devices = range(lax.axis_size(axis))
    route = [(i - distance, i) for i in devices if i - distance in devices]
    return lax.ppermute(block, axis, route)


def attend_rows(q_ref, k_src, fe_row_ref, fe_col_ref, out_ref, out_start, k_start, first, lo, scale):
    window = QROWS + FILE_MOST - lo
    k_window = k_src[0][pl.ds(pl.multiple_of(k_start + lo, TRIM), window), :]
    v_window = k_src[1][pl.ds(pl.multiple_of(k_start + lo, TRIM), window), :]
    q_pos = first + lax.broadcasted_iota(jnp.int32, (QROWS, 1), 0)
    q_doc = jnp.sum((fe_row_ref[...] <= q_pos).astype(jnp.float32), axis=1, keepdims=True)
    k_pos = first - FILE_MOST + lo + lax.broadcasted_iota(jnp.int32, (1, window), 1)
    k_doc = jnp.sum((fe_col_ref[...] <= k_pos).astype(jnp.float32), axis=0, keepdims=True)
    k_doc = jnp.where(k_pos >= 0, k_doc, -1.0)
    row = lax.broadcasted_iota(jnp.int32, (QROWS, window), 0)
    col = lax.broadcasted_iota(jnp.int32, (QROWS, window), 1)
    allowed = (k_doc == q_doc) & (col + lo <= row + FILE_MOST)
    for g in range(q_ref.shape[1] // HD):
        q_head = q_ref[:, g * HD : (g + 1) * HD]
        scores = (
            lax.dot_general(
                q_head, k_window, (((1,), (1,)), ((), ())), preferred_element_type=jnp.float32
            )
            * scale
        )
        scores = jnp.where(allowed, scores, -jnp.inf)
        row_max = jnp.max(scores, axis=1, keepdims=True)
        expo = jnp.exp(scores - row_max)
        weights = (expo / jnp.sum(expo, axis=1, keepdims=True)).astype(jnp.bfloat16)
        result = jnp.dot(weights, v_window, preferred_element_type=jnp.float32)
        out_ref[pl.ds(out_start, QROWS), g * HD : (g + 1) * HD] = result.astype(out_ref.dtype)


def later_kernel(offset_ref, trim_ref, q_ref, k_ref, v_ref, fe_row_ref, fe_col_ref, o_ref, *, scale, skip):
    step = pl.program_id(0)
    block = step + skip
    k_start = pl.multiple_of(block * QROWS - FILE_MOST, QROWS)
    first = offset_ref[0] + block * QROWS
    for t in range(TRIMS + 1):
        pl.when(trim_ref[block] == t)(
            functools.partial(
                attend_rows, q_ref, (k_ref, v_ref), fe_row_ref, fe_col_ref, o_ref, 0, k_start, first,
                t * TRIM, scale,
            )
        )


def early_kernel(owner_ref, offset_ref, trim_ref, q_ref, k_ref, v_ref, rim_ref, fe_row_ref, fe_col_ref,
                 later_ref, o_ref, wide_k, wide_v, attended, *, scale, piece):
    step = pl.program_id(0)
    lead = wide_k.shape[0] - FILE_MOST

    @pl.when(step == 0)
    def _():
        wide_k[0:FILE_MOST, :] = rim_ref[:, 0:HD]
        wide_k[FILE_MOST:, :] = k_ref[0:lead, :]
        wide_v[0:FILE_MOST, :] = rim_ref[:, HD : 2 * HD]
        wide_v[FILE_MOST:, :] = v_ref[0:lead, :]
        attended[lead:, :] = later_ref[lead:, :]

    start = pl.multiple_of(step * QROWS, QROWS)
    first = offset_ref[0] + step * QROWS
    for t in range(TRIMS + 1):
        pl.when(trim_ref[step] == t)(
            functools.partial(
                attend_rows, q_ref, (wide_k, wide_v), fe_row_ref, fe_col_ref, attended, start, start,
                first, t * TRIM, scale,
            )
        )

    @pl.when(step == pl.num_programs(0) - 1)
    def _():
        for p in range(o_ref.shape[0]):
            o_ref[owner_ref[p]] = attended[p * piece : (p + 1) * piece, :]


def leading_trims(offset, file_ends, block_count):
    firsts = offset + QROWS * jnp.arange(block_count, dtype=jnp.int32)
    starts = jnp.max(jnp.where(file_ends[None, :] <= firsts[:, None], file_ends[None, :], 0), axis=1)
    lasts = firsts[:, None] - FILE_MOST + TRIM - 1 + TRIM * jnp.arange(TRIMS, dtype=jnp.int32)[None, :]
    return jnp.sum((lasts < starts[:, None]).astype(jnp.int32), axis=1)

def attend_ordered(owner_row, offset, queries, keys, values, rim, file_ends, scale):
    tok_rows, width = queries.shape
    shard_count = owner_row.shape[0]
    piece = tok_rows // shard_count
    block_count = tok_rows // QROWS
    early = FILE_MOST // QROWS
    trims = leading_trims(offset, file_ends, block_count)
    offset_row = jnp.reshape(offset, (1,))
    fe_row = file_ends.reshape(1, -1)
    fe_col = file_ends.reshape(-1, 1)
    full = lambda shape: pl.BlockSpec(shape, lambda i, *_: (0,) * len(shape))
    params = pltpu.CompilerParams(dimension_semantics=("arbitrary",))
    later = pl.pallas_call(
        functools.partial(later_kernel, scale=scale, skip=early),
        grid_spec=pltpu.PrefetchScalarGridSpec(
            num_scalar_prefetch=2,
            grid=(block_count - early,),
            in_specs=[
                pl.BlockSpec((QROWS, width), lambda i, *_: (i + early, 0)),
                full(keys.shape), full(values.shape), full(fe_row.shape), full(fe_col.shape),
            ],
            out_specs=pl.BlockSpec((QROWS, width), lambda i, *_: (i + early, 0)),
        ),
        out_shape=jax.ShapeDtypeStruct((tok_rows, width), queries.dtype),
        compiler_params=params,
    )(offset_row, trims, queries, keys, values, fe_row, fe_col)
    return pl.pallas_call(
        functools.partial(early_kernel, scale=scale, piece=piece),
        grid_spec=pltpu.PrefetchScalarGridSpec(
            num_scalar_prefetch=3,
            grid=(early,),
            in_specs=[
                pl.BlockSpec((QROWS, width), lambda i, *_: (i, 0)),
                full(keys.shape), full(values.shape), full(rim.shape),
                full(fe_row.shape), full(fe_col.shape), full(later.shape),
            ],
            out_specs=full((shard_count, piece, width)),
            scratch_shapes=[
                pltpu.VMEM((2 * FILE_MOST, HD), keys.dtype),
                pltpu.VMEM((2 * FILE_MOST, HD), values.dtype),
                pltpu.VMEM((tok_rows, width), queries.dtype),
            ],
        ),
        out_shape=jax.ShapeDtypeStruct((shard_count, piece, width), queries.dtype),
        compiler_params=params,
    )(owner_row, offset_row, trims, queries, keys, values, rim, fe_row, fe_col, later)


def per_device(queries, keys, values, file_lengths, owner_of):
    tok_rows = queries.shape[0]
    heads_here = keys.shape[1] // HD
    shard_count = lax.axis_size("seq")
    head_count = lax.axis_size("head")
    offset = lax.axis_index("seq") * tok_rows
    sequence = lax.axis_index("head") * heads_here // KV_HEADS
    rim = from_behind(
        jnp.concatenate([keys[tok_rows - FILE_MOST :], values[tok_rows - FILE_MOST :]], axis=1),
        "seq",
        1,
    )
    file_count = file_lengths.shape[1]
    batch_pick = (jnp.arange(file_lengths.shape[0], dtype=jnp.int32) == sequence).astype(jnp.int32)
    lengths_here = jnp.sum(file_lengths * batch_pick[:, None], axis=0)
    file_index = jnp.arange(file_count, dtype=jnp.int32)
    upto = (file_index[:, None] <= file_index[None, :]).astype(jnp.int32)
    file_ends = jnp.sum(lengths_here[:, None] * upto, axis=0)
    scale = 1.0 / math.sqrt(HD)
    ordered = attend_ordered(
        owner_of[0].astype(jnp.int32),
        offset.astype(jnp.int32),
        queries,
        keys,
        values,
        rim,
        file_ends,
        scale,
    )
    rows_each = ordered.shape[1] // head_count
    chunks = ordered.reshape(shard_count * head_count, rows_each, ordered.shape[2])
    arrived = lax.all_to_all(chunks, ("seq", "head"), 0, 0, tiled=True)
    arrived = arrived.reshape(shard_count, head_count, rows_each, ordered.shape[2])
    arrived = jnp.transpose(arrived, (0, 2, 1, 3)).reshape(
        shard_count, rows_each, head_count * ordered.shape[2]
    )
    return arrived[None]


def solution(mesh):
    return jax.shard_map(
        per_device,
        mesh=mesh,
        in_specs=(P("seq", "head"), P("seq", "head"), P("seq", "head"), P(), P("seq", None)),
        out_specs=P("seq", None, "head", None),
        check_vma=False,
    )
```

time: 124 us -> 123 us (level)
  blocking collectives: 93.2 us -> 89.7 us
  Pallas kernels: 16.2 us -> 18.6 us
    all_to_all x1, blocking collectives: 93.2 us -> 89.7 us  [per_device(): arrived = lax.all_to_all(chunks, ('seq', 'head'), 0, 0, tiled=True)]
    pallas_call x1 -> x2, Pallas kernels: 16.2 us -> 18.6 us  [the longest x1 10.8 us: attend_ordered(): pl.pallas_call(functools.partial(later_kernel, scale=scale, skip=early),...]
  transfers between devices with their start and end apart: 1 -> 1, of which waited for: 1 -> 0; matrix products, arithmetic and copies ran while one was open for 3% -> 3% of each run, Pallas kernels for 0% -> 9%
where the time goes in v6:
time: 123 us
  blocking collectives  89.7 us (73%)
  Pallas kernels  18.6 us (15%)
  local copies, waits for them, and re-layouts  8.79 us (7%)
  starting transfers between devices  3.95 us (3%)
  other arithmetic  1.82 us (1%)
    all_to_all x1, blocking collectives, per_device(): arrived = lax.all_to_all(chunks, ('seq', 'head'), 0, 0, tiled=True)  89.7 us
    pallas_call x1, Pallas kernels, attend_ordered(): pl.pallas_call(functools.partial(later_kernel, scale=scale, skip=early),...  10.8 us
    pallas_call x1, Pallas kernels, attend_ordered(): pl.pallas_call(functools.partial(early_kernel, scale=scale, piece=piece),...  7.82 us
    ppermute x1, starting transfers between devices, from_behind(): return lax.ppermute(block, axis, route)  3.95 us
    reshape x1, local copies, waits for them, and re-layouts, per_device(): ordered.reshape(shard_count * head_count, rows_each, ordered.shape[2])  2.5 us
  transfers between devices with their start and end apart: 1, of which 0 were waited for; matrix products, arithmetic and copies ran while one was open for 3% of the time, Pallas kernels for 9%

profile of v6, /device:TPU:1, one launch (start us, length us, event | category | flops | bytes accessed | tf_op | source)
XLA Modules:
  0.0 123.0 jit_solution(5737800552636387435)
XLA Ops:
  0.0 0.9 slice.6
  0.9 0.9 slice.7
  1.9 3.9 %collective-permute-start = (bf16[512,256]{1,0:T(8,128)(2,1)S(1)}, bf16[512,256]{1,0:T(8,128)(2,1)S(1)}, u32[]{:S(2)}, u32[]{:S(2)}) collective-permute-start(bf16[512,256]{1,0:T(8,128)(2,1)S(1)} %pad_maximum_fusion), channel_id=1, source_target_pairs={{0,24},{24,48},{48,72},{72,96},{96,120},{120,144},{144,168},{168,1... | collective-permute-start | bytes 786440 | tf_op jit(solution)/shard_map/ppermute | solution.py:22
  5.9 0.8 multiply_reduce_fusion
  6.7 0.1 select_reduce_fusion
  6.8 0.6 broadcast_in_dim.9.fe_row_ref
  7.4 0.8 reshape.42.fe_col_ref
  8.2 0.2 select_reduce_fusion.1
  8.4 0.7 fusion.trim_ref
  9.1 10.8 %shard_map.55.later_ref = bf16[1536,512]{1,0:T(8,128)(2,1)} custom-call(s32[1]{0:T(128)} %bitcast.1.offset_ref, s32[6]{0:T(128)} %fusion.trim_ref, bf16[1536,512]{1,0:T(8,128)(2,1)} %q_ref.3, bf16[1536,128]{1,0:T(8,128)(2,1)} %k_ref.3, bf16[1536,128]{1,0:T(8,128)(2,1)} %v_ref.3, s32[1,384]{1,0:T(1,128)} %broadcast_in_dim.9.fe_row_ref, ...), custom_call_target="tpu_custom_call" | custom-call | tf_op jit(solution)/shard_map/pallas_call | solution.py:114
  19.8 0.0 collective-permute-done.rim_ref
  19.9 0.0 copy-start
  19.9 0.7 copy-done
  20.6 7.8 %shard_map.56 = bf16[32,48,512]{2,1,0:T(8,128)(2,1)} custom-call(s32[32]{0:T(128)} %bitcast.10, s32[1]{0:T(128)} %bitcast.1.offset_ref, s32[6]{0:T(128)} %fusion.trim_ref, bf16[1536,512]{1,0:T(8,128)(2,1)} %q_ref.3, bf16[1536,128]{1,0:T(8,128)(2,1)} %k_ref.3, bf16[1536,128]{1,0:T(8,128)(2,1)} %v_ref.3, bf16[512,256]{1,0:T(8,128)(2,1)} %copy-done, ...), custom_call_target="tpu_custom_call" | custom-call | tf_op jit(solution)/shard_map/pallas_call | solution.py:128
  28.4 2.5 %reshape.40 = bf16[768,2,512]{2,1,0:T(2,128)(2,1)S(1)} reshape(bf16[32,48,512]{2,1,0:T(8,128)(2,1)} %shard_map.56) | data formatting | bytes 3145728 | tf_op jit(solution)/shard_map/reshape | solution.py:180
  30.9 89.7 %all_to_all.5 = bf16[768,2,512]{2,1,0:T(2,128)(2,1)S(1)} all-to-all(bf16[768,2,512]{2,1,0:T(2,128)(2,1)S(1)} %reshape.40), channel_id=1, replica_groups=mesh['seq'=32,'head'=24] {'seq','head'}, dimensions={0} | all-to-all | bytes 3145728 | tf_op jit(solution)/shard_map/all_to_all | solution.py:181
  120.6 0.3 copy.14
  120.9 2.1 %broadcast_in_dim_reshape.3 = bf16[1,32,2,12288]{3,2,1,0:T(2,128)(2,1)} reshape(bf16[32,2,24,512]{3,2,1,0:T(8,128)(2,1)S(1)} %bitcast.9) | data formatting | bytes 3145728 | tf_op jit(solution)/shard_map/broadcast_in_dim;reshape | solution.py:186
  (5 shorter events, 0.0 us)
Async XLA Ops:
  1.9 18.0 %collective-permute-start = (bf16[512,256]{1,0:T(8,128)(2,1)S(1)}, bf16[512,256]{1,0:T(8,128)(2,1)S(1)}, u32[]{:S(2)}, u32[]{:S(2)}) collective-permute-start(bf16[512,256]{1,0:T(8,128)(2,1)S(1)} %pad_maximum_fusion), channel_id=1, source_target_pairs={{0,24},{24,48},{48,72},{72,96},{96,120},{120,144},{144,168},{168,1... | collective-permute-start | bytes 786440 | tf_op jit(solution)/shard_map/ppermute | solution.py:22
  19.9 0.7 copy-start

commit v7 on v6

--- a/solution.py
+++ b/solution.py
@@ -177,10 +177,12 @@
         scale,
     )
     rows_each = ordered.shape[1] // head_count
-    chunks = ordered.reshape(shard_count * head_count, rows_each, ordered.shape[2])
-    arrived = lax.all_to_all(chunks, ("seq", "head"), 0, 0, tiled=True)
-    arrived = arrived.reshape(shard_count, head_count, rows_each, ordered.shape[2])
-    arrived = jnp.transpose(arrived, (0, 2, 1, 3)).reshape(
+    chunks = jnp.transpose(
+        ordered.reshape(shard_count, head_count, rows_each, ordered.shape[2]), (1, 0, 2, 3)
+    ).reshape(head_count * shard_count, rows_each, ordered.shape[2])
+    arrived = lax.all_to_all(chunks, ("head", "seq"), 0, 0, tiled=True)
+    arrived = arrived.reshape(head_count, shard_count, rows_each, ordered.shape[2])
+    arrived = jnp.transpose(arrived, (1, 2, 0, 3)).reshape(
         shard_count, rows_each, head_count * ordered.shape[2]
     )
     return arrived[None]

time: 123 us -> 126 us (1.024)
  local copies, waits for them, and re-layouts: 8.79 us -> 12.2 us
    reshape x2 -> x3, local copies, waits for them, and re-layouts: 2.83 us -> 5.16 us  [the longest x2 3.54 us: per_device(): ordered.reshape(shard_count, head_count, rows_each, ordered.shape[2])]
    another operation x1 -> x2, local copies, waits for them, and re-layouts: 2.05 us -> 2.92 us  [per_device(): return arrived[None]]
where the time goes in v7:
time: 126 us
  blocking collectives  89.1 us (71%)
  Pallas kernels  18.6 us (15%)
  local copies, waits for them, and re-layouts  12.2 us (10%)
  starting transfers between devices  3.95 us (3%)
  other arithmetic  1.82 us (1%)
    all_to_all x1, blocking collectives, per_device(): arrived = lax.all_to_all(chunks, ('head', 'seq'), 0, 0, tiled=True)  89.1 us
    pallas_call x1, Pallas kernels, attend_ordered(): pl.pallas_call(functools.partial(later_kernel, scale=scale, skip=early),...  10.8 us
    pallas_call x1, Pallas kernels, attend_ordered(): pl.pallas_call(functools.partial(early_kernel, scale=scale, piece=piece),...  7.83 us
    ppermute x1, starting transfers between devices, from_behind(): return lax.ppermute(block, axis, route)  3.95 us
    reshape x2, local copies, waits for them, and re-layouts, per_device(): ordered.reshape(shard_count, head_count, rows_each, ordered.shape[2])  3.54 us
    another operation x2, local copies, waits for them, and re-layouts, per_device(): return arrived[None]  2.92 us
  transfers between devices with their start and end apart: 1, of which 0 were waited for; matrix products, arithmetic and copies ran while one was open for 3% of the time, Pallas kernels for 9%

profile of v7, /device:TPU:1, one launch (start us, length us, event | category | flops | bytes accessed | tf_op | source)
XLA Modules:
  0.0 125.9 jit_solution(9268469953399648442)
XLA Ops:
  0.0 0.9 slice.6
  0.9 0.9 slice.7
  1.9 3.9 %collective-permute-start = (bf16[512,256]{1,0:T(8,128)(2,1)S(1)}, bf16[512,256]{1,0:T(8,128)(2,1)S(1)}, u32[]{:S(2)}, u32[]{:S(2)}) collective-permute-start(bf16[512,256]{1,0:T(8,128)(2,1)S(1)} %pad_maximum_fusion), channel_id=1, source_target_pairs={{0,24},{24,48},{48,72},{72,96},{96,120},{120,144},{144,168},{168,1... | collective-permute-start | bytes 786440 | tf_op jit(solution)/shard_map/ppermute | solution.py:22
  5.9 0.8 multiply_reduce_fusion
  6.7 0.1 select_reduce_fusion
  6.8 0.6 broadcast_in_dim.9.fe_row_ref
  7.4 0.8 reshape.46.fe_col_ref
  8.2 0.2 select_reduce_fusion.1
  8.4 0.7 fusion.trim_ref
  9.1 10.8 %shard_map.55.later_ref = bf16[1536,512]{1,0:T(8,128)(2,1)} custom-call(s32[1]{0:T(128)} %bitcast.1.offset_ref, s32[6]{0:T(128)} %fusion.trim_ref, bf16[1536,512]{1,0:T(8,128)(2,1)} %q_ref.3, bf16[1536,128]{1,0:T(8,128)(2,1)} %k_ref.3, bf16[1536,128]{1,0:T(8,128)(2,1)} %v_ref.3, s32[1,384]{1,0:T(1,128)} %broadcast_in_dim.9.fe_row_ref, ...), custom_call_target="tpu_custom_call" | custom-call | tf_op jit(solution)/shard_map/pallas_call | solution.py:114
  19.8 0.0 collective-permute-done.rim_ref
  19.8 0.0 copy-start
  19.9 0.7 copy-done
  20.5 7.8 %shard_map.56 = bf16[32,48,512]{2,1,0:T(8,128)(2,1)} custom-call(s32[32]{0:T(128)} %bitcast.12, s32[1]{0:T(128)} %bitcast.1.offset_ref, s32[6]{0:T(128)} %fusion.trim_ref, bf16[1536,512]{1,0:T(8,128)(2,1)} %q_ref.3, bf16[1536,128]{1,0:T(8,128)(2,1)} %k_ref.3, bf16[1536,128]{1,0:T(8,128)(2,1)} %v_ref.3, bf16[512,256]{1,0:T(8,128)(2,1)} %copy-done, ...), custom_call_target="tpu_custom_call" | custom-call | tf_op jit(solution)/shard_map/pallas_call | solution.py:128
  28.4 2.7 %reshape.43 = bf16[32,24,2,512]{3,2,1,0:T(2,128)(2,1)S(1)} reshape(bf16[32,48,512]{2,1,0:T(8,128)(2,1)} %shard_map.56) | data formatting | bytes 3145728 | tf_op jit(solution)/shard_map/reshape | solution.py:181
  31.1 0.9 copy.23
  31.9 1.6 %copy.24 = bf16[768,2,512]{2,1,0:T(2,128)(2,1)S(1)} copy(bf16[768,2,512]{2,0,1:T(8,128)(2,1)S(1)} %bitcast.10) | data formatting | bytes 3145728 | tf_op jit(solution)/shard_map/reshape | solution.py:182
  33.6 89.1 %all_to_all.5 = bf16[768,2,512]{2,1,0:T(2,128)(2,1)S(1)} all-to-all(bf16[768,2,512]{2,1,0:T(2,128)(2,1)S(1)} %copy.24), channel_id=1, replica_groups=mesh['seq'=32,'head'=24] {'head','seq'}, dimensions={0} | all-to-all | bytes 3145728 | tf_op jit(solution)/shard_map/all_to_all | solution.py:183
  122.7 0.2 copy.25
  122.9 0.9 copy.28
  123.8 2.1 %reshape.47 = bf16[1,32,2,12288]{3,2,1,0:T(2,128)(2,1)} reshape(bf16[32,2,24,512]{3,2,1,0:T(8,128)(2,1)S(1)} %copy.28) | data formatting | bytes 3145728 | tf_op jit(solution)/shard_map/broadcast_in_dim;reshape | solution.py:188
  (5 shorter events, 0.0 us)
Async XLA Ops:
  1.9 18.0 %collective-permute-start = (bf16[512,256]{1,0:T(8,128)(2,1)S(1)}, bf16[512,256]{1,0:T(8,128)(2,1)S(1)}, u32[]{:S(2)}, u32[]{:S(2)}) collective-permute-start(bf16[512,256]{1,0:T(8,128)(2,1)S(1)} %pad_maximum_fusion), channel_id=1, source_target_pairs={{0,24},{24,48},{48,72},{72,96},{96,120},{120,144},{144,168},{168,1... | collective-permute-start | bytes 786440 | tf_op jit(solution)/shard_map/ppermute | solution.py:22
  19.8 0.7 copy-start

commit v8 on v6

--- a/solution.py
+++ b/solution.py
@@ -67,7 +67,7 @@
 def early_kernel(owner_ref, offset_ref, trim_ref, q_ref, k_ref, v_ref, rim_ref, fe_row_ref, fe_col_ref,
                  later_ref, o_ref, wide_k, wide_v, attended, *, scale, piece):
     step = pl.program_id(0)
-    lead = wide_k.shape[0] - FILE_MOST
+    lead = attended.shape[0]
 
     @pl.when(step == 0)
     def _():
@@ -75,7 +75,6 @@
         wide_k[FILE_MOST:, :] = k_ref[0:lead, :]
         wide_v[0:FILE_MOST, :] = rim_ref[:, HD : 2 * HD]
         wide_v[FILE_MOST:, :] = v_ref[0:lead, :]
-        attended[lead:, :] = later_ref[lead:, :]
 
     start = pl.multiple_of(step * QROWS, QROWS)
     first = offset_ref[0] + step * QROWS
@@ -90,7 +89,35 @@
     @pl.when(step == pl.num_programs(0) - 1)
     def _():
         for p in range(o_ref.shape[0]):
-            o_ref[owner_ref[p]] = attended[p * piece : (p + 1) * piece, :]
+            top, bottom = p * piece, (p + 1) * piece
+            slot = owner_ref[p]
+            if bottom <= lead:
+                o_ref[slot] = attended[top:bottom, :]
+            elif top >= lead:
+                o_ref[slot] = later_ref[top:bottom, :]
+            else:
+                o_ref[slot, 0 : lead - top, :] = attended[top:lead, :]
+                o_ref[slot, lead - top : piece, :] = later_ref[lead:bottom, :]
+
+
+def rim_kernel(k_ref, v_ref, o_ref):
+    o_ref[:, 0:HD] = k_ref[...]
+    o_ref[:, HD : 2 * HD] = v_ref[...]
+
+
+def rim_of(keys, values):
+    tok_rows = keys.shape[0]
+    last = tok_rows // FILE_MOST - 1
+    return pl.pallas_call(
+        rim_kernel,
+        grid=(1,),
+        in_specs=[
+            pl.BlockSpec((FILE_MOST, HD), lambda i: (last, 0)),
+            pl.BlockSpec((FILE_MOST, HD), lambda i: (last, 0)),
+        ],
+        out_specs=pl.BlockSpec((FILE_MOST, 2 * HD), lambda i: (0, 0)),
+        out_shape=jax.ShapeDtypeStruct((FILE_MOST, 2 * HD), keys.dtype),
+    )(keys, values)
 
 
 def leading_trims(offset, file_ends, block_count):
@@ -139,7 +166,7 @@
             scratch_shapes=[
                 pltpu.VMEM((2 * FILE_MOST, HD), keys.dtype),
                 pltpu.VMEM((2 * FILE_MOST, HD), values.dtype),
-                pltpu.VMEM((tok_rows, width), queries.dtype),
+                pltpu.VMEM((FILE_MOST, width), queries.dtype),
             ],
         ),
         out_shape=jax.ShapeDtypeStruct((shard_count, piece, width), queries.dtype),
@@ -154,11 +181,7 @@
     head_count = lax.axis_size("head")
     offset = lax.axis_index("seq") * tok_rows
     sequence = lax.axis_index("head") * heads_here // KV_HEADS
-    rim = from_behind(
-        jnp.concatenate([keys[tok_rows - FILE_MOST :], values[tok_rows - FILE_MOST :]], axis=1),
-        "seq",
-        1,
-    )
+    rim = from_behind(rim_of(keys, values), "seq", 1)
     file_count = file_lengths.shape[1]
     batch_pick = (jnp.arange(file_lengths.shape[0], dtype=jnp.int32) == sequence).astype(jnp.int32)
     lengths_here = jnp.sum(file_lengths * batch_pick[:, None], axis=0)

time: 123 us -> 123 us (level)
  local copies, waits for them, and re-layouts: 8.79 us -> 6.96 us
    slice x2 -> x0, local copies, waits for them, and re-layouts: 1.83 us -> none  [the longest x1 0.92 us: per_device(): values[tok_rows - FILE_MOST:]]
    pallas_call x0 -> x1, Pallas kernels: none -> 1.7 us  [rim_of(): pl.pallas_call(rim_kernel, grid=(1,), in_specs=[pl.BlockSpec((FILE_MOST,...]
  transfers between devices with their start and end apart: 1 -> 1, of which waited for: 0 -> 0; matrix products, arithmetic and copies ran while one was open for 3% -> 3% of each run, Pallas kernels for 9% -> 8%
where the time goes in v8:
time: 123 us
  blocking collectives  90.1 us (73%)
  Pallas kernels  19.8 us (16%)
  local copies, waits for them, and re-layouts  6.96 us (6%)
  starting transfers between devices  3.94 us (3%)
  other arithmetic  1.79 us (1%)
    all_to_all x1, blocking collectives, per_device(): arrived = lax.all_to_all(chunks, ('seq', 'head'), 0, 0, tiled=True)  90.1 us
    pallas_call x1, Pallas kernels, attend_ordered(): pl.pallas_call(functools.partial(later_kernel, scale=scale, skip=early),...  10.4 us
    pallas_call x1, Pallas kernels, attend_ordered(): pl.pallas_call(functools.partial(early_kernel, scale=scale, piece=piece),...  7.75 us
    ppermute x1, starting transfers between devices, from_behind(): return lax.ppermute(block, axis, route)  3.94 us
    reshape x1, local copies, waits for them, and re-layouts, per_device(): ordered.reshape(shard_count * head_count, rows_each, ordered.shape[2])  2.5 us
  transfers between devices with their start and end apart: 1, of which 0 were waited for; matrix products, arithmetic and copies ran while one was open for 3% of the time, Pallas kernels for 8%

profile of v8, /device:TPU:1, one launch (start us, length us, event | category | flops | bytes accessed | tf_op | source)
XLA Modules:
  0.0 122.7 jit_solution(2798188728534065720)
XLA Ops:
  0.0 1.7 %shard_map.55 = bf16[512,256]{1,0:T(8,128)(2,1)} custom-call(bf16[1536,128]{1,0:T(8,128)(2,1)} %k_ref.5, bf16[1536,128]{1,0:T(8,128)(2,1)} %v_ref.5), custom_call_target="tpu_custom_call" | custom-call | tf_op jit(solution)/shard_map/pallas_call | solution.py:111
  1.7 3.9 %collective-permute-start = (bf16[512,256]{1,0:T(8,128)(2,1)}, bf16[512,256]{1,0:T(8,128)(2,1)S(1)}, u32[]{:S(2)}, u32[]{:S(2)}) collective-permute-start(bf16[512,256]{1,0:T(8,128)(2,1)} %shard_map.55), channel_id=1, source_target_pairs={{0,24},{24,48},{48,72},{72,96},{96,120},{120,144},{144,168},{168,1... | collective-permute-start | bytes 786440 | tf_op jit(solution)/shard_map/ppermute | solution.py:22
  5.7 0.8 multiply_reduce_fusion
  6.5 0.1 select_reduce_fusion
  6.6 0.6 broadcast_in_dim.9.fe_row_ref
  7.2 0.8 reshape.42.fe_col_ref
  8.0 0.2 select_reduce_fusion.1
  8.2 0.7 fusion.trim_ref
  8.9 10.4 %shard_map.56.later_ref = bf16[1536,512]{1,0:T(8,128)(2,1)} custom-call(s32[1]{0:T(128)} %bitcast.1.offset_ref, s32[6]{0:T(128)} %fusion.trim_ref, bf16[1536,512]{1,0:T(8,128)(2,1)} %q_ref.3, bf16[1536,128]{1,0:T(8,128)(2,1)} %k_ref.5, bf16[1536,128]{1,0:T(8,128)(2,1)} %v_ref.5, s32[1,384]{1,0:T(1,128)} %broadcast_in_dim.9.fe_row_ref, ...), custom_call_target="tpu_custom_call" | custom-call | tf_op jit(solution)/shard_map/pallas_call | solution.py:141
  19.2 0.0 collective-permute-done.rim_ref
  19.2 0.0 copy-start
  19.2 0.7 copy-done
  19.9 7.8 %shard_map.57 = bf16[32,48,512]{2,1,0:T(8,128)(2,1)} custom-call(s32[32]{0:T(128)} %bitcast.10, s32[1]{0:T(128)} %bitcast.1.offset_ref, s32[6]{0:T(128)} %fusion.trim_ref, bf16[1536,512]{1,0:T(8,128)(2,1)} %q_ref.3, bf16[1536,128]{1,0:T(8,128)(2,1)} %k_ref.5, bf16[1536,128]{1,0:T(8,128)(2,1)} %v_ref.5, bf16[512,256]{1,0:T(8,128)(2,1)} %copy-done, ...), custom_call_target="tpu_custom_call" | custom-call | tf_op jit(solution)/shard_map/pallas_call | solution.py:155
  27.7 2.5 %reshape.40 = bf16[768,2,512]{2,1,0:T(2,128)(2,1)S(1)} reshape(bf16[32,48,512]{2,1,0:T(8,128)(2,1)} %shard_map.57) | data formatting | bytes 3145728 | tf_op jit(solution)/shard_map/reshape | solution.py:203
  30.2 90.1 %all_to_all.5 = bf16[768,2,512]{2,1,0:T(2,128)(2,1)S(1)} all-to-all(bf16[768,2,512]{2,1,0:T(2,128)(2,1)S(1)} %reshape.40), channel_id=1, replica_groups=mesh['seq'=32,'head'=24] {'seq','head'}, dimensions={0} | all-to-all | bytes 3145728 | tf_op jit(solution)/shard_map/all_to_all | solution.py:204
  120.3 0.3 copy.14
  120.6 2.1 %broadcast_in_dim_reshape.3 = bf16[1,32,2,12288]{3,2,1,0:T(2,128)(2,1)} reshape(bf16[32,2,24,512]{3,2,1,0:T(8,128)(2,1)S(1)} %bitcast.9) | data formatting | bytes 3145728 | tf_op jit(solution)/shard_map/broadcast_in_dim;reshape | solution.py:209
  (4 shorter events, 0.0 us)
Async XLA Ops:
  1.7 17.5 %collective-permute-start = (bf16[512,256]{1,0:T(8,128)(2,1)}, bf16[512,256]{1,0:T(8,128)(2,1)S(1)}, u32[]{:S(2)}, u32[]{:S(2)}) collective-permute-start(bf16[512,256]{1,0:T(8,128)(2,1)} %shard_map.55), channel_id=1, source_target_pairs={{0,24},{24,48},{48,72},{72,96},{96,120},{120,144},{144,168},{168,1... | collective-permute-start | bytes 786440 | tf_op jit(solution)/shard_map/ppermute | solution.py:22
  19.2 0.7 copy-start

commit v9 on v8

--- a/solution.py
+++ b/solution.py
@@ -50,22 +50,34 @@
         out_ref[pl.ds(out_start, QROWS), g * HD : (g + 1) * HD] = result.astype(out_ref.dtype)
 
 
-def later_kernel(offset_ref, trim_ref, q_ref, k_ref, v_ref, fe_row_ref, fe_col_ref, o_ref, *, scale, skip):
+def later_kernel(owner_ref, offset_ref, trim_ref, q_ref, k_ref, v_ref, fe_row_ref, fe_col_ref, o_ref,
+                 attended, *, scale, skip, piece):
     step = pl.program_id(0)
     block = step + skip
+    lead = skip * QROWS
     k_start = pl.multiple_of(block * QROWS - FILE_MOST, QROWS)
     first = offset_ref[0] + block * QROWS
     for t in range(TRIMS + 1):
         pl.when(trim_ref[block] == t)(
             functools.partial(
-                attend_rows, q_ref, (k_ref, v_ref), fe_row_ref, fe_col_ref, o_ref, 0, k_start, first,
-                t * TRIM, scale,
+                attend_rows, q_ref, (k_ref, v_ref), fe_row_ref, fe_col_ref, attended,
+                pl.multiple_of(step * QROWS, QROWS), k_start, first, t * TRIM, scale,
             )
         )
 
+    @pl.when(step == pl.num_programs(0) - 1)
+    def _():
+        for p in range(o_ref.shape[0]):
+            top, bottom = p * piece, (p + 1) * piece
+            if top >= lead:
+                o_ref[owner_ref[p]] = attended[top - lead : bottom - lead, :]
+            elif bottom > lead:
+                o_ref[owner_ref[p], lead - top : piece, :] = attended[0 : bottom - lead, :]
+
 
 def early_kernel(owner_ref, offset_ref, trim_ref, q_ref, k_ref, v_ref, rim_ref, fe_row_ref, fe_col_ref,
-                 later_ref, o_ref, wide_k, wide_v, attended, *, scale, piece):
+                 later_ref, o_ref, wide_k, wide_v, attended, sems, *, scale, piece):
+    del later_ref
     step = pl.program_id(0)
     lead = attended.shape[0]
 
@@ -88,16 +100,21 @@
 
     @pl.when(step == pl.num_programs(0) - 1)
     def _():
+        copies = []
         for p in range(o_ref.shape[0]):
-            top, bottom = p * piece, (p + 1) * piece
-            slot = owner_ref[p]
-            if bottom <= lead:
-                o_ref[slot] = attended[top:bottom, :]
-            elif top >= lead:
-                o_ref[slot] = later_ref[top:bottom, :]
-            else:
-                o_ref[slot, 0 : lead - top, :] = attended[top:lead, :]
-                o_ref[slot, lead - top : piece, :] = later_ref[lead:bottom, :]
+            top, bottom = p * piece, min((p + 1) * piece, lead)
+            if top < lead:
+                copies.append(
+                    pltpu.make_async_copy(
+                        attended.at[top:bottom, :],
+                        o_ref.at[owner_ref[p], 0 : bottom - top, :],
+                        sems.at[p],
+                    )
+                )
+        for copy in copies:
+            copy.start()
+        for copy in copies:
+            copy.wait()
 
 
 def rim_kernel(k_ref, v_ref, o_ref):
@@ -139,19 +156,20 @@
     full = lambda shape: pl.BlockSpec(shape, lambda i, *_: (0,) * len(shape))
     params = pltpu.CompilerParams(dimension_semantics=("arbitrary",))
     later = pl.pallas_call(
-        functools.partial(later_kernel, scale=scale, skip=early),
+        functools.partial(later_kernel, scale=scale, skip=early, piece=piece),
         grid_spec=pltpu.PrefetchScalarGridSpec(
-            num_scalar_prefetch=2,
+            num_scalar_prefetch=3,
             grid=(block_count - early,),
             in_specs=[
                 pl.BlockSpec((QROWS, width), lambda i, *_: (i + early, 0)),
                 full(keys.shape), full(values.shape), full(fe_row.shape), full(fe_col.shape),
             ],
-            out_specs=pl.BlockSpec((QROWS, width), lambda i, *_: (i + early, 0)),
+            out_specs=full((shard_count, piece, width)),
+            scratch_shapes=[pltpu.VMEM((tok_rows - early * QROWS, width), queries.dtype)],
         ),
-        out_shape=jax.ShapeDtypeStruct((tok_rows, width), queries.dtype),
+        out_shape=jax.ShapeDtypeStruct((shard_count, piece, width), queries.dtype),
         compiler_params=params,
-    )(offset_row, trims, queries, keys, values, fe_row, fe_col)
+    )(owner_row, offset_row, trims, queries, keys, values, fe_row, fe_col)
     return pl.pallas_call(
         functools.partial(early_kernel, scale=scale, piece=piece),
         grid_spec=pltpu.PrefetchScalarGridSpec(
@@ -160,16 +178,18 @@
             in_specs=[
                 pl.BlockSpec((QROWS, width), lambda i, *_: (i, 0)),
                 full(keys.shape), full(values.shape), full(rim.shape),
-                full(fe_row.shape), full(fe_col.shape), full(later.shape),
+                full(fe_row.shape), full(fe_col.shape), pl.BlockSpec(memory_space=pl.ANY),
             ],
-            out_specs=full((shard_count, piece, width)),
+            out_specs=pl.BlockSpec(memory_space=pl.ANY),
             scratch_shapes=[
                 pltpu.VMEM((2 * FILE_MOST, HD), keys.dtype),
                 pltpu.VMEM((2 * FILE_MOST, HD), values.dtype),
-                pltpu.VMEM((FILE_MOST, width), queries.dtype),
+                pltpu.VMEM((early * QROWS, width), queries.dtype),
+                pltpu.SemaphoreType.DMA((shard_count,)),
             ],
         ),
         out_shape=jax.ShapeDtypeStruct((shard_count, piece, width), queries.dtype),
+        input_output_aliases={9: 0},
         compiler_params=params,
     )(owner_row, offset_row, trims, queries, keys, values, rim, fe_row, fe_col, later)
 

time: 123 us -> 123 us (level)
  transfers between devices with their start and end apart: 1 -> 1, of which waited for: 0 -> 0; matrix products, arithmetic and copies ran while one was open for 3% -> 3% of each run, Pallas kernels for 8% -> 9%
where the time goes in v9:
time: 123 us; the launch traced here: 122 us
  blocking collectives  89.5 us (73%)
  Pallas kernels  20 us (16%)
  local copies, waits for them, and re-layouts  6.97 us (6%)
  starting transfers between devices  3.94 us (3%)
  other arithmetic  1.73 us (1%)
    all_to_all x1, blocking collectives, per_device(): arrived = lax.all_to_all(chunks, ('seq', 'head'), 0, 0, tiled=True)  89.5 us
    pallas_call x1, Pallas kernels, attend_ordered(): pl.pallas_call(functools.partial(later_kernel, scale=scale, skip=early, p...  11.3 us
    pallas_call x1, Pallas kernels, attend_ordered(): pl.pallas_call(functools.partial(early_kernel, scale=scale, piece=piece),...  7.02 us
    ppermute x1, starting transfers between devices, from_behind(): return lax.ppermute(block, axis, route)  3.94 us
    reshape x1, local copies, waits for them, and re-layouts, per_device(): ordered.reshape(shard_count * head_count, rows_each, ordered.shape[2])  2.5 us
  transfers between devices with their start and end apart: 1, of which 0 were waited for; matrix products, arithmetic and copies ran while one was open for 3% of the time, Pallas kernels for 9%

profile of v9, /device:TPU:1, one launch (start us, length us, event | category | flops | bytes accessed | tf_op | source)
XLA Modules:
  0.0 122.2 jit_solution(4405998372172412680)
XLA Ops:
  0.0 1.7 %shard_map.55 = bf16[512,256]{1,0:T(8,128)(2,1)} custom-call(bf16[1536,128]{1,0:T(8,128)(2,1)} %k_ref.5, bf16[1536,128]{1,0:T(8,128)(2,1)} %v_ref.5), custom_call_target="tpu_custom_call" | custom-call | tf_op jit(solution)/shard_map/pallas_call | solution.py:128
  1.7 3.9 %collective-permute-start = (bf16[512,256]{1,0:T(8,128)(2,1)}, bf16[512,256]{1,0:T(8,128)(2,1)S(1)}, u32[]{:S(2)}, u32[]{:S(2)}) collective-permute-start(bf16[512,256]{1,0:T(8,128)(2,1)} %shard_map.55), channel_id=1, source_target_pairs={{0,24},{24,48},{48,72},{72,96},{96,120},{120,144},{144,168},{168,1... | collective-permute-start | bytes 786440 | tf_op jit(solution)/shard_map/ppermute | solution.py:22
  5.7 0.8 multiply_reduce_fusion
  6.5 0.1 select_reduce_fusion
  6.6 0.6 broadcast_in_dim.9.fe_row_ref
  7.2 0.8 reshape.42.fe_col_ref
  8.0 0.2 select_reduce_fusion.1
  8.2 0.6 fusion.trim_ref
  8.8 11.3 %shard_map.56.later_ref = bf16[32,48,512]{2,1,0:T(8,128)(2,1)} custom-call(s32[32]{0:T(128)} %bitcast.10, s32[1]{0:T(128)} %bitcast.1.offset_ref, s32[6]{0:T(128)} %fusion.trim_ref, bf16[1536,512]{1,0:T(8,128)(2,1)} %q_ref.3, bf16[1536,128]{1,0:T(8,128)(2,1)} %k_ref.5, bf16[1536,128]{1,0:T(8,128)(2,1)} %v_ref.5, s32[1,384]{1,0:T(1,128)} %broadcast_in_dim.9.fe_row_ref, ...), custom_call_target="tpu_custom_call" | custom-call | tf_op jit(solution)/shard_map/pallas_call | solution.py:158
  20.1 0.0 collective-permute-done.rim_ref
  20.1 0.0 copy-start
  20.1 0.7 copy-done
  20.8 7.0 %shard_map.57 = bf16[32,48,512]{2,1,0:T(8,128)(2,1)} custom-call(s32[32]{0:T(128)} %bitcast.11, s32[1]{0:T(128)} %bitcast.1.offset_ref, s32[6]{0:T(128)} %fusion.trim_ref, bf16[1536,512]{1,0:T(8,128)(2,1)} %q_ref.3, bf16[1536,128]{1,0:T(8,128)(2,1)} %k_ref.5, bf16[1536,128]{1,0:T(8,128)(2,1)} %v_ref.5, ...), custom_call_target="tpu_custom_call", output_to_operand_aliasing={{}: (9, {})} | custom-call | tf_op jit(solution)/shard_map/pallas_call | solution.py:173
  27.8 2.5 %reshape.40 = bf16[768,2,512]{2,1,0:T(2,128)(2,1)S(1)} reshape(bf16[32,48,512]{2,1,0:T(8,128)(2,1)} %shard_map.57) | data formatting | bytes 3145728 | tf_op jit(solution)/shard_map/reshape | solution.py:223
  30.3 89.5 %all_to_all.5 = bf16[768,2,512]{2,1,0:T(2,128)(2,1)S(1)} all-to-all(bf16[768,2,512]{2,1,0:T(2,128)(2,1)S(1)} %reshape.40), channel_id=1, replica_groups=mesh['seq'=32,'head'=24] {'seq','head'}, dimensions={0} | all-to-all | bytes 3145728 | tf_op jit(solution)/shard_map/all_to_all | solution.py:224
  119.8 0.3 copy.15
  120.2 2.1 %broadcast_in_dim_reshape.3 = bf16[1,32,2,12288]{3,2,1,0:T(2,128)(2,1)} reshape(bf16[32,2,24,512]{3,2,1,0:T(8,128)(2,1)S(1)} %bitcast.9) | data formatting | bytes 3145728 | tf_op jit(solution)/shard_map/broadcast_in_dim;reshape | solution.py:229
  (4 shorter events, 0.0 us)
Async XLA Ops:
  1.7 18.4 %collective-permute-start = (bf16[512,256]{1,0:T(8,128)(2,1)}, bf16[512,256]{1,0:T(8,128)(2,1)S(1)}, u32[]{:S(2)}, u32[]{:S(2)}) collective-permute-start(bf16[512,256]{1,0:T(8,128)(2,1)} %shard_map.55), channel_id=1, source_target_pairs={{0,24},{24,48},{48,72},{72,96},{96,120},{120,144},{144,168},{168,1... | collective-permute-start | bytes 786440 | tf_op jit(solution)/shard_map/ppermute | solution.py:22
  20.1 0.7 copy-start

commit v10 on v9

--- a/solution.py
+++ b/solution.py
@@ -29,7 +29,12 @@
     q_pos = first + lax.broadcasted_iota(jnp.int32, (QROWS, 1), 0)
     q_doc = jnp.sum((fe_row_ref[...] <= q_pos).astype(jnp.float32), axis=1, keepdims=True)
     k_pos = first - FILE_MOST + lo + lax.broadcasted_iota(jnp.int32, (1, window), 1)
-    k_doc = jnp.sum((fe_col_ref[...] <= k_pos).astype(jnp.float32), axis=0, keepdims=True)
+    k_pos_col = first - FILE_MOST + lo + lax.broadcasted_iota(jnp.int32, (window, 1), 0)
+    ended = (fe_row_ref[...] <= k_pos_col).astype(jnp.bfloat16)
+    ones = jnp.ones((8, ended.shape[1]), jnp.bfloat16)
+    k_doc = lax.dot_general(
+        ones, ended, (((1,), (1,)), ((), ())), preferred_element_type=jnp.float32
+    )[0:1]
     k_doc = jnp.where(k_pos >= 0, k_doc, -1.0)
     row = lax.broadcasted_iota(jnp.int32, (QROWS, window), 0)
     col = lax.broadcasted_iota(jnp.int32, (QROWS, window), 1)

time: 123 us -> 123 us (level)
  transfers between devices with their start and end apart: 1 -> 1, of which waited for: 0 -> 0; matrix products, arithmetic and copies ran while one was open for 3% -> 3% of each run, Pallas kernels for 9% -> 10%
where the time goes in v10:
time: 123 us
  blocking collectives  89.5 us (73%)
  Pallas kernels  20.6 us (17%)
  local copies, waits for them, and re-layouts  6.97 us (6%)
  starting transfers between devices  3.94 us (3%)
  other arithmetic  1.73 us (1%)
    all_to_all x1, blocking collectives, per_device(): arrived = lax.all_to_all(chunks, ('seq', 'head'), 0, 0, tiled=True)  89.5 us
    pallas_call x1, Pallas kernels, attend_ordered(): pl.pallas_call(functools.partial(later_kernel, scale=scale, skip=early, p...  11.7 us
    pallas_call x1, Pallas kernels, attend_ordered(): pl.pallas_call(functools.partial(early_kernel, scale=scale, piece=piece),...  7.2 us
    ppermute x1, starting transfers between devices, from_behind(): return lax.ppermute(block, axis, route)  3.94 us
    reshape x1, local copies, waits for them, and re-layouts, per_device(): ordered.reshape(shard_count * head_count, rows_each, ordered.shape[2])  2.5 us
  transfers between devices with their start and end apart: 1, of which 0 were waited for; matrix products, arithmetic and copies ran while one was open for 3% of the time, Pallas kernels for 10%

profile of v10, /device:TPU:1, one launch (start us, length us, event | category | flops | bytes accessed | tf_op | source)
XLA Modules:
  0.0 122.9 jit_solution(11676296382348113976)
XLA Ops:
  0.0 1.7 %shard_map.55 = bf16[512,256]{1,0:T(8,128)(2,1)} custom-call(bf16[1536,128]{1,0:T(8,128)(2,1)} %k_ref.5, bf16[1536,128]{1,0:T(8,128)(2,1)} %v_ref.5), custom_call_target="tpu_custom_call" | custom-call | tf_op jit(solution)/shard_map/pallas_call | solution.py:133
  1.7 3.9 %collective-permute-start = (bf16[512,256]{1,0:T(8,128)(2,1)}, bf16[512,256]{1,0:T(8,128)(2,1)S(1)}, u32[]{:S(2)}, u32[]{:S(2)}) collective-permute-start(bf16[512,256]{1,0:T(8,128)(2,1)} %shard_map.55), channel_id=1, source_target_pairs={{0,24},{24,48},{48,72},{72,96},{96,120},{120,144},{144,168},{168,1... | collective-permute-start | bytes 786440 | tf_op jit(solution)/shard_map/ppermute | solution.py:22
  5.7 0.8 multiply_reduce_fusion
  6.5 0.1 select_reduce_fusion
  6.6 0.6 broadcast_in_dim.9.fe_row_ref
  7.2 0.8 reshape.42.fe_col_ref
  8.0 0.2 select_reduce_fusion.1
  8.2 0.6 fusion.trim_ref
  8.8 11.7 %shard_map.56.later_ref = bf16[32,48,512]{2,1,0:T(8,128)(2,1)} custom-call(s32[32]{0:T(128)} %bitcast.10, s32[1]{0:T(128)} %bitcast.1.offset_ref, s32[6]{0:T(128)} %fusion.trim_ref, bf16[1536,512]{1,0:T(8,128)(2,1)} %q_ref.3, bf16[1536,128]{1,0:T(8,128)(2,1)} %k_ref.5, bf16[1536,128]{1,0:T(8,128)(2,1)} %v_ref.5, s32[1,384]{1,0:T(1,128)} %broadcast_in_dim.9.fe_row_ref, ...), custom_call_target="tpu_custom_call" | custom-call | tf_op jit(solution)/shard_map/pallas_call | solution.py:163
  20.6 0.0 collective-permute-done.rim_ref
  20.6 0.0 copy-start
  20.6 0.7 copy-done
  21.3 7.2 %shard_map.57 = bf16[32,48,512]{2,1,0:T(8,128)(2,1)} custom-call(s32[32]{0:T(128)} %bitcast.11, s32[1]{0:T(128)} %bitcast.1.offset_ref, s32[6]{0:T(128)} %fusion.trim_ref, bf16[1536,512]{1,0:T(8,128)(2,1)} %q_ref.3, bf16[1536,128]{1,0:T(8,128)(2,1)} %k_ref.5, bf16[1536,128]{1,0:T(8,128)(2,1)} %v_ref.5, ...), custom_call_target="tpu_custom_call", output_to_operand_aliasing={{}: (9, {})} | custom-call | tf_op jit(solution)/shard_map/pallas_call | solution.py:178
  28.5 2.5 %reshape.40 = bf16[768,2,512]{2,1,0:T(2,128)(2,1)S(1)} reshape(bf16[32,48,512]{2,1,0:T(8,128)(2,1)} %shard_map.57) | data formatting | bytes 3145728 | tf_op jit(solution)/shard_map/reshape | solution.py:228
  31.0 89.5 %all_to_all.5 = bf16[768,2,512]{2,1,0:T(2,128)(2,1)S(1)} all-to-all(bf16[768,2,512]{2,1,0:T(2,128)(2,1)S(1)} %reshape.40), channel_id=1, replica_groups=mesh['seq'=32,'head'=24] {'seq','head'}, dimensions={0} | all-to-all | bytes 3145728 | tf_op jit(solution)/shard_map/all_to_all | solution.py:229
  120.5 0.3 copy.15
  120.8 2.1 %broadcast_in_dim_reshape.3 = bf16[1,32,2,12288]{3,2,1,0:T(2,128)(2,1)} reshape(bf16[32,2,24,512]{3,2,1,0:T(8,128)(2,1)S(1)} %bitcast.9) | data formatting | bytes 3145728 | tf_op jit(solution)/shard_map/broadcast_in_dim;reshape | solution.py:234
  (4 shorter events, 0.0 us)
Async XLA Ops:
  1.7 18.9 %collective-permute-start = (bf16[512,256]{1,0:T(8,128)(2,1)}, bf16[512,256]{1,0:T(8,128)(2,1)S(1)}, u32[]{:S(2)}, u32[]{:S(2)}) collective-permute-start(bf16[512,256]{1,0:T(8,128)(2,1)} %shard_map.55), channel_id=1, source_target_pairs={{0,24},{24,48},{48,72},{72,96},{96,120},{120,144},{144,168},{168,1... | collective-permute-start | bytes 786440 | tf_op jit(solution)/shard_map/ppermute | solution.py:22
  20.6 0.7 copy-start
